TPU v7x, 768 devices: a whole 4x8x12 slice. The times are simulated.
768 devices in a mesh: row: 192 (over z_lo, y, x, core), col: 4 (over z_hi).
Axes of the slice: x: 4, y: 8, z: 12 (z_hi: 4, z_lo: 3; z = z_hi * 3 + z_lo), core: 2. Of those that a mesh axis runs over, the one named last changes fastest.
Arguments:
- features: bfloat16 [98304, 512], P('row', 'col'), may hold values from -6 to 6
- out_grad: bfloat16 [98304, 512], P('row', 'col'), may hold values from -6 to 6
- self_weight: bfloat16 [512, 512], replicated, may hold values from -0.25 to 0.25
- neigh_weight: bfloat16 [512, 512], replicated, may hold values from -1 to 1
- tile_rows: int32 [98304, 16, 128], P('row'), may hold values from 0 to 1, as said below
- tile_cols: int32 [98304, 16], P('row'), may hold values from 0 to 767, as said below
- degree: int32 [98304], P('row'), may hold values from 32 to 512
Outputs:
- output: bfloat16 [98304, 512], P('row', 'col')
- feature_grad: bfloat16 [98304, 512], P('row', 'col')
Inputs may be any that keep to these rules, and one draw needn't show every extreme that they name: Entries are 0 or 1. The adjacency built from tile_rows and tile_cols is symmetric. All nodes of one block of 128 nodes have the same tile_cols. A slot that is not used holds an all-zero tile. `tile_cols`: for each slot, block a names block b exactly when block b names block a; b differs from a by 1 or 2, or b equals a and that slot's tile is all zero.
All inputs are finite; a program needn't handle non-finite values.
Results may differ from a plain program's by a relative error of at most 0.0034.
Values may be sent and summed in bfloat16 or wider, within the bound.
No kernel may reach another device: no remote copies, remote signals or barrier semaphores. Data moves between devices by JAX's collectives and lax.ppermute only.
A program may use at most 128 MiB of HBM per device.

v0:
```python
import jax
import jax.numpy as jnp
from jax import lax
from jax.sharding import PartitionSpec as P


def passed_along(block, axis, distance):
    devices = range(lax.axis_size(axis))
    route = [(i - distance, i) for i in devices if i - distance in devices]
    return lax.ppermute(block, axis, route)


def cross_dot(left, right):
    return lax.dot_general(
        left, right, (((1,), (1,)), ((), ())), preferred_element_type=jnp.float32
    )


def per_device(features, out_grad, self_weight, neigh_weight, tile_rows, tile_cols, degree):
    rows_here, part = features.shape
    block = tile_rows.shape[2]
    inverse = 1.0 / degree.astype(jnp.float32)
    scaled = (out_grad.astype(jnp.float32) * inverse[:, None]).astype(jnp.bfloat16)
    received = {}
    for offset in (2, 1, -1, -2):
        received[offset] = passed_along((features, scaled), "row", offset)
    feat_panel = jnp.concatenate(
        [received[2][0], received[1][0], features, received[-1][0], received[-2][0]], axis=0
    )
    grad_panel = jnp.concatenate(
        [received[2][1], received[1][1], scaled, received[-1][1], received[-2][1]], axis=0
    )
    first_block = (lax.axis_index("row") - 2) * (rows_here // block)
    window_blocks = feat_panel.shape[0] // block
    local_cols = tile_cols - first_block
    owner = (
        local_cols[:, :, None] == jnp.arange(window_blocks, dtype=jnp.int32)[None, None, :]
    ).astype(jnp.bfloat16)
    slab = jnp.einsum(
        "rkn,rkb->rnb", owner, tile_rows.astype(jnp.bfloat16), preferred_element_type=jnp.float32
    )
    slab = slab.astype(jnp.bfloat16).reshape(rows_here, window_blocks * block)
    feat_sum = jnp.dot(slab, feat_panel, preferred_element_type=jnp.float32)
    grad_sum = jnp.dot(slab, grad_panel, preferred_element_type=jnp.float32)
    aggregated = (feat_sum * inverse[:, None]).astype(jnp.bfloat16)
    back_agg = grad_sum.astype(jnp.bfloat16)
    offset = lax.axis_index("col") * part
    self_rows = lax.dynamic_slice_in_dim(self_weight, offset, part, 0)
    neigh_rows = lax.dynamic_slice_in_dim(neigh_weight, offset, part, 0)
    self_cols = lax.dynamic_slice_in_dim(self_weight, offset, part, 1)
    neigh_cols = lax.dynamic_slice_in_dim(neigh_weight, offset, part, 1)
    forward_terms = jnp.dot(features, self_rows, preferred_element_type=jnp.float32) + jnp.dot(
        aggregated, neigh_rows, preferred_element_type=jnp.float32
    )
    backward_terms = cross_dot(out_grad, self_cols) + cross_dot(back_agg, neigh_cols)
    output, feature_grad = (
        lax.psum_scatter(forward_terms, "col", scatter_dimension=1, tiled=True),
        lax.psum_scatter(backward_terms, "col", scatter_dimension=1, tiled=True),
    )
    return (output.astype(jnp.bfloat16), feature_grad.astype(jnp.bfloat16))


def solution(mesh):
    placed = (
        P("row", "col"),
        P("row", "col"),
        P(),
        P(),
        P("row", None, None),
        P("row", None),
        P("row"),
    )
    return jax.shard_map(
        per_device,
        mesh=mesh,
        in_specs=placed,
        out_specs=(P("row", "col"), P("row", "col")),
        check_vma=False,
    )
```

profile of v0, /device:TPU:1, one launch (start us, length us, event | category | flops | bytes accessed | tf_op | source)
XLA Modules:
  0.0 157.5 jit_solution(1210131312592569879)
XLA Ops:
  7.2 4.7 %collective-permute-start = (bf16[512,128]{1,0:T(8,128)(2,1)}, bf16[512,128]{1,0:T(8,128)(2,1)}, u32[]{:S(2)}, u32[]{:S(2)}) collective-permute-start(bf16[512,128]{1,0:T(8,128)(2,1)} %param.7), channel_id=1, source_target_pairs={{0,8},{4,12},{8,16},{12,20},{16,24},{20,28},{24,32},{28,36},{32,40... | collective-permute-start | bytes 393224 | tf_op jit(solution)/shard_map/ppermute | solution.py:10
  11.9 3.3 %collective-permute-start.1 = (bf16[512,128]{1,0:T(8,128)(2,1)}, bf16[512,128]{1,0:T(8,128)(2,1)}, u32[]{:S(2)}, u32[]{:S(2)}) collective-permute-start(bf16[512,128]{1,0:T(8,128)(2,1)} %param.7), channel_id=1, source_target_pairs={{0,4},{4,8},{8,12},{12,16},{16,20},{20,24},{24,28},{28,32},{32,36}... | collective-permute-start | bytes 393224 | tf_op jit(solution)/shard_map/ppermute | solution.py:10
  15.3 8.3 %collective-permute-start.2 = (bf16[512,128]{1,0:T(8,128)(2,1)}, bf16[512,128]{1,0:T(8,128)(2,1)S(1)}, u32[]{:S(2)}, u32[]{:S(2)}) collective-permute-start(bf16[512,128]{1,0:T(8,128)(2,1)} %param.7), channel_id=1, source_target_pairs={{4,0},{8,4},{12,8},{16,12},{20,16},{24,20},{28,24},{32,28},{36,32}... | collective-permute-start | bytes 393224 | tf_op jit(solution)/shard_map/ppermute | solution.py:10
  23.6 1.3 collective-permute-start.3
  24.9 0.8 broadcast_subtract_fusion
  25.8 2.2 %convolution_bitcast_fusion.1 = f32[512,512]{0,1:T(8,128)} fusion(bf16[512,128]{1,0:T(8,128)(2,1)} %param.7, bf16[512,512]{1,0:T(8,128)(2,1)S(1)} %copy-done, s32[]{:T(128)S(6)} %select_n.2), kind=kOutput, calls=%fused_computation.8 | convolution fusion | flops 67108864 | bytes 1310724 | tf_op jit(solution)/shard_map/dot_general | solution.py:52
  28.1 6.7 %fusion.1 = bf16[512,20,128]{2,1,0:T(8,128)(2,1)} fusion(s32[512,16,128]{2,1,0:T(8,128)} %param.11, s32[512,16]{1,0:T(8,128)S(1)} %copy.14), kind=kOutput, calls=%fused_computation.2 | convolution fusion | flops 44466176 | bytes 6848512 | tf_op jit(solution)/shard_map/rkn,rkb->rnb/dot_general | solution.py:39
  34.8 3.7 %copy.15 = bf16[512,20,128]{0,2,1:T(8,128)(2,1)S(1)} copy(bf16[512,20,128]{2,1,0:T(8,128)(2,1)} %fusion.1) | data formatting | bytes 5242880 | tf_op jit(solution)/shard_map/convert_element_type | solution.py:42
  38.6 0.9 constant_dynamic-update-slice_fusion.4
  39.5 0.9 constant_dynamic-update-slice_fusion.3
  40.5 0.8 copy-done.2
  41.4 3.8 %convolution_add_fusion.1 = f32[512,512]{0,1:T(8,128)} fusion(f32[512,512]{0,1:T(8,128)} %convolution_bitcast_fusion.1, bf16[512,2560]{0,1:T(8,128)(2,1)S(1)} %bitcast.11, bf16[2560,128]{1,0:T(8,128)(2,1)} %copy-done.2, bf16[512,512]{1,0:T(8,128)(2,1)} %param.10, s32[]{:T(128)S(6)} %select_n.2, f32[512]{0:T(512)S(1)} %convert_divide_fusion), kind=kOutput, calls=%fused_computation.7 | convolution fusion | flops 403046400 | bytes 5507076 | tf_op jit(solution)/shard_map/dot_general | solution.py:52
  45.4 4.0 %collective-permute-start.4 = (bf16[512,128]{1,0:T(8,128)(2,1)S(1)}, bf16[512,128]{1,0:T(8,128)(2,1)S(1)}, u32[]{:S(2)}, u32[]{:S(2)}) collective-permute-start(bf16[512,128]{1,0:T(8,128)(2,1)S(1)} %multiply_convert_fusion), channel_id=1, source_target_pairs={{0,8},{4,12},{8,16},{12,20},{16,24},{20,28},{24,32},{28,36},{32,40... | collective-permute-start | bytes 393224 | tf_op jit(solution)/shard_map/ppermute | solution.py:10
  49.4 1.9 %collective-permute-start.5 = (bf16[512,128]{1,0:T(8,128)(2,1)S(1)}, bf16[512,128]{1,0:T(8,128)(2,1)S(1)}, u32[]{:S(2)}, u32[]{:S(2)}) collective-permute-start(bf16[512,128]{1,0:T(8,128)(2,1)S(1)} %multiply_convert_fusion), channel_id=1, source_target_pairs={{0,4},{4,8},{8,12},{12,16},{16,20},{20,24},{24,28},{28,32},{32,36}... | collective-permute-start | bytes 393224 | tf_op jit(solution)/shard_map/ppermute | solution.py:10
  51.4 2.4 %collective-permute-start.6 = (bf16[512,128]{1,0:T(8,128)(2,1)S(1)}, bf16[512,128]{1,0:T(8,128)(2,1)S(1)}, u32[]{:S(2)}, u32[]{:S(2)}) collective-permute-start(bf16[512,128]{1,0:T(8,128)(2,1)S(1)} %multiply_convert_fusion), channel_id=1, source_target_pairs={{4,0},{8,4},{12,8},{16,12},{20,16},{24,20},{28,24},{32,28},{36,32}... | collective-permute-start | bytes 393224 | tf_op jit(solution)/shard_map/ppermute | solution.py:10
  53.8 1.3 collective-permute-start.7
  55.1 1.3 convolution_bitcast_fusion
  57.7 0.8 constant_dynamic-update-slice_fusion.7
  59.1 2.0 %collective-permute-done.7 = bf16[512,128]{1,0:T(8,128)(2,1)S(1)} collective-permute-done((bf16[512,128]{1,0:T(8,128)(2,1)S(1)}, bf16[512,128]{1,0:T(8,128)(2,1)S(1)}, u32[]{:S(2)}, u32[]{:S(2)}) %collective-permute-start.7) | collective-permute-done | bytes 131104 | tf_op jit(solution)/shard_map/ppermute | solution.py:10
  61.8 3.8 %convolution_add_fusion = f32[512,512]{0,1:T(8,128)} fusion(f32[512,512]{0,1:T(8,128)} %convolution_bitcast_fusion, bf16[512,2560]{0,1:T(8,128)(2,1)S(1)} %bitcast.12, bf16[2560,128]{1,0:T(8,128)(2,1)} %constant_dynamic-update-slice_fusion.5, bf16[512,512]{1,0:T(8,128)(2,1)} %param.10, s32[]{:T(128)S(6)} %select_n.2), kind=kOutput, calls=%fused_computation.5 | convolution fusion | flops 402980864 | bytes 5505028 | tf_op jit(solution)/shard_map/dot_general | solution.py:14
  65.6 28.3 %reduce-scatter.3.cloned.1.call-done = f32[512,128]{0,1:T(8,128)} async-done(((f32[512,512]{0,1:T(8,128)}), f32[512,128]{0,1:T(8,128)}) %reduce-scatter.3.cloned.1.call-update) | async-done | bytes 262160 | tf_op jit(solution)/shard_map/reduce_scatter | solution.py:57
  93.9 1.0 convert_element_type.32
  95.6 53.3 %reduce-scatter.5.cloned.1.call-done = f32[512,128]{0,1:T(8,128)} async-done(((f32[512,512]{0,1:T(8,128)}), f32[512,128]{0,1:T(8,128)}) %reduce-scatter.5.cloned.1.call-update) | async-done | bytes 262160 | tf_op jit(solution)/shard_map/reduce_scatter | solution.py:58
  149.0 1.0 convert_element_type.36
  (32 shorter events, 4.6 us)
Async XLA Ops:
  7.2 18.7 %copy-start = (bf16[512,512]{1,0:T(8,128)(2,1)S(1)}, bf16[512,512]{1,0:T(8,128)(2,1)}, u32[]{:S(2)}) copy-start(bf16[512,512]{1,0:T(8,128)(2,1)} %param.9) | copy-start | bytes 1572868
  7.2 86.7 %reduce-scatter.3.cloned.1.call-start = ((), (), s32[]{:S(2)}) async-start(), calls=%async_computation.2 | async-start | bytes 1310720 | tf_op jit(solution)/shard_map/reduce_scatter | solution.py:57
  7.2 31.3 %collective-permute-start = (bf16[512,128]{1,0:T(8,128)(2,1)}, bf16[512,128]{1,0:T(8,128)(2,1)}, u32[]{:S(2)}, u32[]{:S(2)}) collective-permute-start(bf16[512,128]{1,0:T(8,128)(2,1)} %param.7), channel_id=1, source_target_pairs={{0,8},{4,12},{8,16},{12,20},{16,24},{20,28},{24,32},{28,36},{32,40... | collective-permute-start | bytes 393224 | tf_op jit(solution)/shard_map/ppermute | solution.py:10
  11.9 27.5 %collective-permute-start.1 = (bf16[512,128]{1,0:T(8,128)(2,1)}, bf16[512,128]{1,0:T(8,128)(2,1)}, u32[]{:S(2)}, u32[]{:S(2)}) collective-permute-start(bf16[512,128]{1,0:T(8,128)(2,1)} %param.7), channel_id=1, source_target_pairs={{0,4},{4,8},{8,12},{12,16},{16,20},{20,24},{24,28},{28,32},{32,36}... | collective-permute-start | bytes 393224 | tf_op jit(solution)/shard_map/ppermute | solution.py:10
  15.3 25.2 %collective-permute-start.2 = (bf16[512,128]{1,0:T(8,128)(2,1)}, bf16[512,128]{1,0:T(8,128)(2,1)S(1)}, u32[]{:S(2)}, u32[]{:S(2)}) collective-permute-start(bf16[512,128]{1,0:T(8,128)(2,1)} %param.7), channel_id=1, source_target_pairs={{4,0},{8,4},{12,8},{16,12},{20,16},{24,20},{28,24},{32,28},{36,32}... | collective-permute-start | bytes 393224 | tf_op jit(solution)/shard_map/ppermute | solution.py:10
  23.6 16.9 %collective-permute-start.3 = (bf16[512,128]{1,0:T(8,128)(2,1)}, bf16[512,128]{1,0:T(8,128)(2,1)S(1)}, u32[]{:S(2)}, u32[]{:S(2)}) collective-permute-start(bf16[512,128]{1,0:T(8,128)(2,1)} %param.7), channel_id=1, source_target_pairs={{8,0},{12,4},{16,8},{20,12},{24,16},{28,20},{32,24},{36,28},{40,32... | collective-permute-start | bytes 393224 | tf_op jit(solution)/shard_map/ppermute | solution.py:10
  28.1 6.8 %copy-start.4 = (s32[512]{0:T(512)S(1)}, s32[512]{0:T(512)}, u32[]{:S(2)}) copy-start(s32[512]{0:T(512)} %param.13) | copy-start | bytes 6148
  34.8 5.6 %copy-start.3 = (bf16[512,128]{1,0:T(8,128)(2,1)S(1)}, bf16[512,128]{1,0:T(8,128)(2,1)}, u32[]{:S(2)}) copy-start(bf16[512,128]{1,0:T(8,128)(2,1)} %param.7) | copy-start | bytes 393220
  40.5 0.9 copy-start.2
  41.4 3.9 %copy-start.1 = (bf16[512,128]{1,0:T(8,128)(2,1)S(1)}, bf16[512,128]{1,0:T(8,128)(2,1)}, u32[]{:S(2)}) copy-start(bf16[512,128]{1,0:T(8,128)(2,1)} %param.8) | copy-start | bytes 393220
  45.2 103.7 %reduce-scatter.5.cloned.1.call-start = ((), (), s32[]{:S(2)}) async-start(), calls=%async_computation.3 | async-start | bytes 1310720 | tf_op jit(solution)/shard_map/reduce_scatter | solution.py:58
  45.4 10.9 %collective-permute-start.4 = (bf16[512,128]{1,0:T(8,128)(2,1)S(1)}, bf16[512,128]{1,0:T(8,128)(2,1)S(1)}, u32[]{:S(2)}, u32[]{:S(2)}) collective-permute-start(bf16[512,128]{1,0:T(8,128)(2,1)S(1)} %multiply_convert_fusion), channel_id=1, source_target_pairs={{0,8},{4,12},{8,16},{12,20},{16,24},{20,28},{24,32},{28,36},{32,40... | collective-permute-start | bytes 393224 | tf_op jit(solution)/shard_map/ppermute | solution.py:10
  49.4 7.6 %collective-permute-start.5 = (bf16[512,128]{1,0:T(8,128)(2,1)S(1)}, bf16[512,128]{1,0:T(8,128)(2,1)S(1)}, u32[]{:S(2)}, u32[]{:S(2)}) collective-permute-start(bf16[512,128]{1,0:T(8,128)(2,1)S(1)} %multiply_convert_fusion), channel_id=1, source_target_pairs={{0,4},{4,8},{8,12},{12,16},{16,20},{20,24},{24,28},{28,32},{32,36}... | collective-permute-start | bytes 393224 | tf_op jit(solution)/shard_map/ppermute | solution.py:10
  51.4 7.1 %collective-permute-start.6 = (bf16[512,128]{1,0:T(8,128)(2,1)S(1)}, bf16[512,128]{1,0:T(8,128)(2,1)S(1)}, u32[]{:S(2)}, u32[]{:S(2)}) collective-permute-start(bf16[512,128]{1,0:T(8,128)(2,1)S(1)} %multiply_convert_fusion), channel_id=1, source_target_pairs={{4,0},{8,4},{12,8},{16,12},{20,16},{24,20},{28,24},{32,28},{36,32}... | collective-permute-start | bytes 393224 | tf_op jit(solution)/shard_map/ppermute | solution.py:10
  53.8 7.3 %collective-permute-start.7 = (bf16[512,128]{1,0:T(8,128)(2,1)S(1)}, bf16[512,128]{1,0:T(8,128)(2,1)S(1)}, u32[]{:S(2)}, u32[]{:S(2)}) collective-permute-start(bf16[512,128]{1,0:T(8,128)(2,1)S(1)} %multiply_convert_fusion), channel_id=1, source_target_pairs={{8,0},{12,4},{16,8},{20,12},{24,16},{28,20},{32,24},{36,28},{40,32... | collective-permute-start | bytes 393224 | tf_op jit(solution)/shard_map/ppermute | solution.py:10
Sparse Core Ops, SparseCore 0:
  45.4 48.4 reduce-scatter.2
  97.0 51.8 reduce-scatter.4
where the time goes:
time: 158 us
  waiting for transfers between devices  83.7 us (53%)
  starting transfers between devices  27.4 us (17%)
  matrix products  17.9 us (11%)
  between operations  14.2 us (9%)
  local copies, waits for them, and re-layouts  10.7 us (7%)
  other arithmetic  3.61 us (2%)
    reduce_scatter x1, waiting for transfers between devices, per_device(): lax.psum_scatter(backward_terms, 'col', scatter_dimension=1, tiled=True)  53.3 us
    reduce_scatter x1, waiting for transfers between devices, per_device(): lax.psum_scatter(forward_terms, 'col', scatter_dimension=1, tiled=True)  28.3 us
    ppermute x8, starting transfers between devices, passed_along(): return lax.ppermute(block, axis, route)  27.3 us
    dot_general x1, matrix products, per_device(): jnp.einsum('rkn,rkb->rnb', owner, tile_rows.astype(jnp.bfloat16), preferr...  6.75 us
    unnamed x19, local copies, waits for them, and re-layouts  6.23 us
    dot_general x2, matrix products, cross_dot(): lax.dot_general(left, right, (((1,), (1,)), ((), ())), preferred_element_...  5.06 us
    dot_general x1, matrix products, per_device(): jnp.dot(aggregated, neigh_rows, preferred_element_type=jnp.float32)  3.83 us
    convert_element_type x1, local copies, waits for them, and re-layouts, per_device(): slab = slab.astype(jnp.bfloat16).reshape(rows_here, window_blocks * block)  3.71 us
  transfers between devices with their start and end apart: 10, of which 3 were waited for; matrix products, arithmetic and copies ran while one was open for 16% of the time, Pallas kernels for 0%

commit v1 on v0

v1 whole, which is shorter than its diff:
```python
import jax
import jax.numpy as jnp
from jax import lax
from jax.sharding import PartitionSpec as P

USE_ALL_TO_ALL = True


def shifted(block, axis, distance):
    devices = range(lax.axis_size(axis))
    route = [(i - distance, i) for i in devices if i - distance in devices]
    return lax.ppermute(block, axis, route)


def swap_chunks(block, axis):
    n = lax.axis_size(axis)
    if USE_ALL_TO_ALL:
        return lax.all_to_all(block, axis, 0, 0, tiled=True)
    m = block.shape[0] // n
    me = lax.axis_index(axis)
    chunks = block.reshape(n, m, block.shape[1])
    got = [None] * n
    got[0] = lax.dynamic_index_in_dim(chunks, me, 0, keepdims=False)
    for s in range(1, n):
        send = lax.dynamic_index_in_dim(chunks, (me + s) % n, 0, keepdims=False)
        got[s] = lax.ppermute(send, axis, [(i, (i + s) % n) for i in range(n)])
    stacked = jnp.stack(got, 0)
    order = (me - jnp.arange(n)) % n
    return jnp.zeros_like(stacked).at[order].set(stacked).reshape(block.shape)


def per_device(features, out_grad, self_weight, neigh_weight, tile_rows, tile_cols, degree):
    rows_here, part = features.shape
    block = tile_rows.shape[2]
    width = self_weight.shape[0]
    n_col = lax.axis_size("col")
    chunk = rows_here // n_col
    inverse = 1.0 / degree.astype(jnp.float32)
    scaled = (out_grad.astype(jnp.float32) * inverse[:, None]).astype(jnp.bfloat16)

    own_in = swap_chunks(jnp.concatenate([features, out_grad], axis=1), "col")

    reach = 2 * block
    pair = jnp.concatenate([features, scaled], axis=1)
    from_prev = shifted(pair[rows_here - reach:], "row", 1)
    from_next = shifted(pair[:reach], "row", -1)
    window = jnp.concatenate([from_prev, pair, from_next], axis=0)
    window_blocks = window.shape[0] // block
    first_block = lax.axis_index("row") * (rows_here // block) - reach // block
    local_cols = tile_cols - first_block
    owner = (
        local_cols[:, :, None] == jnp.arange(window_blocks, dtype=jnp.int32)[None, None, :]
    ).astype(jnp.bfloat16)
    slab = jnp.einsum(
        "rkn,rkb->rnb", owner, tile_rows.astype(jnp.bfloat16), preferred_element_type=jnp.float32
    )
    slab = slab.astype(jnp.bfloat16).reshape(rows_here, window_blocks * block)
    sums = jnp.dot(slab, window, preferred_element_type=jnp.float32)
    aggregated = (sums[:, :part] * inverse[:, None]).astype(jnp.bfloat16)
    back_agg = sums[:, part:].astype(jnp.bfloat16)
    agg_in = swap_chunks(jnp.concatenate([aggregated, back_agg], axis=1), "col")

    own_in = own_in.reshape(n_col, chunk, 2, part)
    agg_in = agg_in.reshape(n_col, chunk, 2, part)
    ws = self_weight.reshape(n_col, part, width)
    wn = neigh_weight.reshape(n_col, part, width)
    ws_t = self_weight.T.reshape(n_col, part, width)
    wn_t = neigh_weight.T.reshape(n_col, part, width)

    def project(x, w):
        return lax.dot_general(
            x, w, (((0, 2), (0, 1)), ((), ())), preferred_element_type=jnp.float32
        )

    output = project(own_in[:, :, 0], ws) + project(agg_in[:, :, 0], wn)
    feature_grad = project(own_in[:, :, 1], ws_t) + project(agg_in[:, :, 1], wn_t)
    both = jnp.stack(
        [output.astype(jnp.bfloat16), feature_grad.astype(jnp.bfloat16)], axis=0
    )
    both = both.reshape(2, chunk, n_col, part).transpose(2, 1, 0, 3).reshape(n_col * chunk, 2 * part)
    back = swap_chunks(both, "col").reshape(rows_here, 2, part)
    return (back[:, 0], back[:, 1])


def solution(mesh):
    placed = (
        P("row", "col"),
        P("row", "col"),
        P(),
        P(),
        P("row", None, None),
        P("row", None),
        P("row"),
    )
    return jax.shard_map(
        per_device,
        mesh=mesh,
        in_specs=placed,
        out_specs=(P("row", "col"), P("row", "col")),
        check_vma=False,
    )
```

time: 158 us -> 82.4 us (0.52)
  the two profiles are of different devices: /device:TPU:1 before, /device:TPU:30 now
where the time goes in v1:
time: 82.4 us; the launch traced here: 81.9 us
  waiting for transfers between devices  27.9 us (34%)
  starting transfers between devices  23.5 us (29%)
  blocking collectives  17.7 us (21%)
  matrix products  4.42 us (5%)
  local copies, waits for them, and re-layouts  4.32 us (5%)
  other arithmetic  3.24 us (4%)
  between operations  0.86 us (1%)
    all_to_all x2, waiting for transfers between devices, swap_chunks(): return lax.all_to_all(block, axis, 0, 0, tiled=True)  27.9 us
    all_to_all x2, starting transfers between devices, swap_chunks(): return lax.all_to_all(block, axis, 0, 0, tiled=True)  17.9 us
    all_to_all x1, blocking collectives, swap_chunks(): return lax.all_to_all(block, axis, 0, 0, tiled=True)  17.7 us
    ppermute x2, starting transfers between devices, shifted(): return lax.ppermute(block, axis, route)  5.56 us
    dot_general x1, matrix products, per_device(): jnp.einsum('rkn,rkb->rnb', owner, tile_rows.astype(jnp.bfloat16), preferr...  2.94 us
    unnamed x9, local copies, waits for them, and re-layouts  2.77 us
    concatenate x1, other arithmetic, per_device(): own_in = swap_chunks(jnp.concatenate([features, out_grad], axis=1), 'col')  1.69 us
  transfers between devices with their start and end apart: 4, of which 2 were waited for; matrix products, arithmetic and copies ran while one was open for 8% of the time, Pallas kernels for 0%

profile of v1, /device:TPU:30, one launch (start us, length us, event | category | flops | bytes accessed | tf_op | source)
XLA Modules:
  0.0 81.9 jit_solution(1413623676428668123)
XLA Ops:
  0.6 0.7 convert_divide_fusion
  1.3 1.0 %copy.30 = bf16[512,128]{0,1:T(8,128)(2,1)S(1)} copy(bf16[512,128]{1,0:T(8,128)(2,1)} %param.8) | data formatting | bytes 262144 | tf_op args[1]
  2.3 1.0 %copy.31 = bf16[512,128]{0,1:T(8,128)(2,1)S(1)} copy(bf16[512,128]{1,0:T(8,128)(2,1)} %param.7) | data formatting | bytes 262144 | tf_op args[0]
  3.4 1.9 %collective-permute-start = (bf16[256,256]{0,1:T(8,128)(2,1)S(1)}, bf16[256,256]{0,1:T(8,128)(2,1)S(1)}, u32[]{:S(2)}, u32[]{:S(2)}) collective-permute-start(bf16[256,256]{0,1:T(8,128)(2,1)S(1)} %get-tuple-element.4), channel_id=1, source_target_pairs={{0,4},{4,8},{8,12},{12,16},{16,20},{20,24},{24,28},{28,32},{32,36}... | collective-permute-start | bytes 393224 | tf_op jit(solution)/shard_map/ppermute | solution.py:12
  5.4 3.6 %collective-permute-start.1 = (bf16[256,256]{0,1:T(8,128)(2,1)S(1)}, bf16[256,256]{0,1:T(8,128)(2,1)S(1)}, u32[]{:S(2)}, u32[]{:S(2)}) collective-permute-start(bf16[256,256]{0,1:T(8,128)(2,1)S(1)} %get-tuple-element.5), channel_id=1, source_target_pairs={{4,0},{8,4},{12,8},{16,12},{20,16},{24,20},{28,24},{32,28},{36,32}... | collective-permute-start | bytes 393224 | tf_op jit(solution)/shard_map/ppermute | solution.py:12
  9.0 1.7 %pad_maximum_fusion = bf16[512,256]{1,0:T(8,128)(2,1)} fusion(bf16[512,128]{1,0:T(8,128)(2,1)} %param.8, bf16[512,128]{1,0:T(8,128)(2,1)} %param.7), kind=kLoop, calls=%fused_computation.27 | loop fusion | flops 524288 | bytes 524288 | tf_op jit(solution)/shard_map/concatenate | solution.py:41
  10.7 14.5 %all-to-all-start = ((bf16[4,128,256]{2,1,0:T(8,128)(2,1)}), bf16[4,128,256]{2,1,0:T(8,128)(2,1)S(1)}, u32[]{:S(2)}, u32[]{:S(2)}) async-start(bf16[4,128,256]{2,1,0:T(8,128)(2,1)} %bitcast), calls=%async_computation | async-start | bytes 524288 | tf_op jit(solution)/shard_map/all_to_all | solution.py:18
  25.3 2.9 %fusion.2 = bf16[512,8,128]{2,1,0:T(8,128)(2,1)S(1)} fusion(s32[512,16,128]{2,1,0:T(8,128)} %param.11, s32[512,16]{1,0:T(8,128)S(1)} %copy.29), kind=kOutput, calls=%fused_computation.3 | convolution fusion | flops 18415616 | bytes 5275648 | tf_op jit(solution)/shard_map/rkn,rkb->rnb/dot_general | solution.py:54
  28.3 0.5 fusion.9
  28.9 0.8 copy_bitcast_fusion
  29.6 11.9 %all-to-all-done = bf16[4,128,256]{2,1,0:T(8,128)(2,1)S(1)} async-done(((bf16[4,128,256]{2,1,0:T(8,128)(2,1)}), bf16[4,128,256]{2,1,0:T(8,128)(2,1)S(1)}, u32[]{:S(2)}, u32[]{:S(2)}) %all-to-all-start) | async-done | bytes 262176 | tf_op jit(solution)/shard_map/all_to_all | solution.py:18
  41.5 3.4 %all-to-all-start.1 = ((bf16[4,128,256]{1,2,0:T(8,128)(2,1)}), bf16[4,128,256]{1,2,0:T(8,128)(2,1)S(1)}, u32[]{:S(2)}, u32[]{:S(2)}) async-start(bf16[4,128,256]{1,2,0:T(8,128)(2,1)} %copy_bitcast_fusion), calls=%async_computation.1 | async-start | bytes 524288 | tf_op jit(solution)/shard_map/all_to_all | solution.py:18
  44.9 0.2 copy.43
  45.2 0.2 copy.42
  45.4 0.2 copy.27
  45.6 16.0 %all-to-all-done.1 = bf16[4,128,256]{1,2,0:T(8,128)(2,1)S(1)} async-done(((bf16[4,128,256]{1,2,0:T(8,128)(2,1)}), bf16[4,128,256]{1,2,0:T(8,128)(2,1)S(1)}, u32[]{:S(2)}, u32[]{:S(2)}) %all-to-all-start.1) | async-done | bytes 262176 | tf_op jit(solution)/shard_map/all_to_all | solution.py:18
  61.6 0.2 convolution_bitcast_fusion
  61.8 0.3 fusion.7
  62.2 0.3 convolution_bitcast_fusion.2
  62.5 0.3 fusion.8
  62.9 17.7 %all_to_all.27 = bf16[4,128,256]{1,2,0:T(8,128)(2,1)S(1)} all-to-all(bf16[4,128,256]{1,2,0:T(8,128)(2,1)S(1)} %bitcast.71), channel_id=1, replica_groups=mesh['row'=192,'col'=4] {'col'}, dimensions={0} | all-to-all | bytes 524288 | tf_op jit(solution)/shard_map/all_to_all | solution.py:18
  80.6 0.1 copy.40
  80.8 0.4 fusion.23
  81.2 0.7 copy_bitcast_fusion.1
  (18 shorter events, 0.6 us)
Async XLA Ops:
  0.6 24.6 %copy-start.2 = (s32[512,16]{0,1:T(8,128)S(1)}, s32[512,16]{0,1:T(8,128)}, u32[]{:S(2)}) copy-start(s32[512,16]{0,1:T(8,128)} %param.12) | copy-start | bytes 98308
  3.4 24.9 %collective-permute-start = (bf16[256,256]{0,1:T(8,128)(2,1)S(1)}, bf16[256,256]{0,1:T(8,128)(2,1)S(1)}, u32[]{:S(2)}, u32[]{:S(2)}) collective-permute-start(bf16[256,256]{0,1:T(8,128)(2,1)S(1)} %get-tuple-element.4), channel_id=1, source_target_pairs={{0,4},{4,8},{8,12},{12,16},{16,20},{20,24},{24,28},{28,32},{32,36}... | collective-permute-start | bytes 393224 | tf_op jit(solution)/shard_map/ppermute | solution.py:12
  5.4 22.9 %collective-permute-start.1 = (bf16[256,256]{0,1:T(8,128)(2,1)S(1)}, bf16[256,256]{0,1:T(8,128)(2,1)S(1)}, u32[]{:S(2)}, u32[]{:S(2)}) collective-permute-start(bf16[256,256]{0,1:T(8,128)(2,1)S(1)} %get-tuple-element.5), channel_id=1, source_target_pairs={{4,0},{8,4},{12,8},{16,12},{20,16},{24,20},{28,24},{32,28},{36,32}... | collective-permute-start | bytes 393224 | tf_op jit(solution)/shard_map/ppermute | solution.py:12
  10.7 30.8 %all-to-all-start = ((bf16[4,128,256]{2,1,0:T(8,128)(2,1)}), bf16[4,128,256]{2,1,0:T(8,128)(2,1)S(1)}, u32[]{:S(2)}, u32[]{:S(2)}) async-start(bf16[4,128,256]{2,1,0:T(8,128)(2,1)} %bitcast), calls=%async_computation | async-start | bytes 524288 | tf_op jit(solution)/shard_map/all_to_all | solution.py:18
  28.3 16.6 %copy-start = (bf16[512,512]{1,0:T(8,128)(2,1)S(1)}, bf16[512,512]{1,0:T(8,128)(2,1)}, u32[]{:S(2)}) copy-start(bf16[512,512]{1,0:T(8,128)(2,1)} %param.10) | copy-start | bytes 1572868
  28.8 16.4 %copy-start.1 = (bf16[512,512]{1,0:T(8,128)(2,1)S(1)}, bf16[512,512]{1,0:T(8,128)(2,1)}, u32[]{:S(2)}) copy-start(bf16[512,512]{1,0:T(8,128)(2,1)} %param.9) | copy-start | bytes 1572868
  41.5 20.1 %all-to-all-start.1 = ((bf16[4,128,256]{1,2,0:T(8,128)(2,1)}), bf16[4,128,256]{1,2,0:T(8,128)(2,1)S(1)}, u32[]{:S(2)}, u32[]{:S(2)}) async-start(bf16[4,128,256]{1,2,0:T(8,128)(2,1)} %copy_bitcast_fusion), calls=%async_computation.1 | async-start | bytes 524288 | tf_op jit(solution)/shard_map/all_to_all | solution.py:18

commit v2 on v1

--- a/solution.py
+++ b/solution.py
@@ -3,7 +3,7 @@
 from jax import lax
 from jax.sharding import PartitionSpec as P
 
-USE_ALL_TO_ALL = True
+USE_ALL_TO_ALL = False
 
 
 def shifted(block, axis, distance):
@@ -19,14 +19,12 @@
     m = block.shape[0] // n
     me = lax.axis_index(axis)
     chunks = block.reshape(n, m, block.shape[1])
-    got = [None] * n
-    got[0] = lax.dynamic_index_in_dim(chunks, me, 0, keepdims=False)
+    got = [lax.dynamic_index_in_dim(chunks, me, 0, keepdims=False)]
     for s in range(1, n):
-        send = lax.dynamic_index_in_dim(chunks, (me + s) % n, 0, keepdims=False)
-        got[s] = lax.ppermute(send, axis, [(i, (i + s) % n) for i in range(n)])
+        send = lax.dynamic_index_in_dim(chunks, (me - s) % n, 0, keepdims=False)
+        got.append(lax.ppermute(send, axis, [(i, (i - s) % n) for i in range(n)]))
     stacked = jnp.stack(got, 0)
-    order = (me - jnp.arange(n)) % n
-    return jnp.zeros_like(stacked).at[order].set(stacked).reshape(block.shape)
+    return jnp.roll(stacked, me, axis=0).reshape(block.shape)
 
 
 def per_device(features, out_grad, self_weight, neigh_weight, tile_rows, tile_cols, degree):

time: 82.4 us -> 86.3 us (1.047)
  the two profiles are of different devices: /device:TPU:30 before, /device:TPU:32 now
where the time goes in v2:
time: 86.3 us; the launch traced here: 85.8 us
  starting transfers between devices  58.8 us (68%)
  waiting for transfers between devices  13.4 us (16%)
  local copies, waits for them, and re-layouts  5.32 us (6%)
  matrix products  4.42 us (5%)
  other arithmetic  2.74 us (3%)
  between operations  1.14 us (1%)
    ppermute x9, starting transfers between devices, swap_chunks(): got.append(lax.ppermute(send, axis, [(i, (i - s) % n) for i in range(n)]))  49.9 us
    ppermute x9, waiting for transfers between devices, swap_chunks(): got.append(lax.ppermute(send, axis, [(i, (i - s) % n) for i in range(n)]))  13.4 us
    ppermute x2, starting transfers between devices, shifted(): return lax.ppermute(block, axis, route)  8.88 us
    unnamed x10, local copies, waits for them, and re-layouts  3.38 us
    dot_general x1, matrix products, per_device(): jnp.einsum('rkn,rkb->rnb', owner, tile_rows.astype(jnp.bfloat16), preferr...  2.94 us
  transfers between devices with their start and end apart: 11, of which 4 were waited for; matrix products, arithmetic and copies ran while one was open for 6% of the time, Pallas kernels for 0%

profile of v2, /device:TPU:32, one launch (start us, length us, event | category | flops | bytes accessed | tf_op | source)
XLA Modules:
  0.0 85.8 jit_solution(13417930339076716503)
XLA Ops:
  0.6 0.7 convert_divide_fusion
  1.3 1.0 %copy.34 = bf16[512,128]{0,1:T(8,128)(2,1)S(1)} copy(bf16[512,128]{1,0:T(8,128)(2,1)} %param.10) | data formatting | bytes 262144 | tf_op args[1]
  2.3 1.0 %copy.35 = bf16[512,128]{0,1:T(8,128)(2,1)S(1)} copy(bf16[512,128]{1,0:T(8,128)(2,1)} %param.9) | data formatting | bytes 262144 | tf_op args[0]
  3.4 1.9 %collective-permute-start.3 = (bf16[256,256]{0,1:T(8,128)(2,1)S(1)}, bf16[256,256]{0,1:T(8,128)(2,1)S(1)}, u32[]{:S(2)}, u32[]{:S(2)}) collective-permute-start(bf16[256,256]{0,1:T(8,128)(2,1)S(1)} %get-tuple-element.17), channel_id=1, source_target_pairs={{0,4},{4,8},{8,12},{12,16},{16,20},{20,24},{24,28},{28,32},{32,36}... | collective-permute-start | bytes 393224 | tf_op jit(solution)/shard_map/ppermute | solution.py:12
  5.4 7.0 %collective-permute-start.4 = (bf16[256,256]{0,1:T(8,128)(2,1)S(1)}, bf16[256,256]{0,1:T(8,128)(2,1)S(1)}, u32[]{:S(2)}, u32[]{:S(2)}) collective-permute-start(bf16[256,256]{0,1:T(8,128)(2,1)S(1)} %get-tuple-element.18), channel_id=1, source_target_pairs={{4,0},{8,4},{12,8},{16,12},{20,16},{24,20},{28,24},{32,28},{36,32}... | collective-permute-start | bytes 393224 | tf_op jit(solution)/shard_map/ppermute | solution.py:12
  12.4 1.0 %pad_maximum_fusion = bf16[512,256]{1,0:T(8,128)(2,1)S(1)} fusion(bf16[512,128]{1,0:T(8,128)(2,1)} %param.10, bf16[512,128]{1,0:T(8,128)(2,1)} %param.9), kind=kLoop, calls=%fused_computation.71 | loop fusion | flops 524288 | bytes 524288 | tf_op jit(solution)/shard_map/concatenate | solution.py:39
  13.4 14.6 %collective-permute-start = (bf16[128,256]{1,0:T(8,128)(2,1)S(1)}, bf16[128,256]{1,0:T(8,128)(2,1)S(1)}, u32[]{:S(2)}, u32[]{:S(2)}) collective-permute-start(bf16[128,256]{1,0:T(8,128)(2,1)S(1)} %get-tuple-element.11), channel_id=1, source_target_pairs={{0,3},{1,0},{2,1},{3,2},{4,7},{5,4},{6,5},{7,6},{8,11},{9,8},{10,9... | collective-permute-start | bytes 196616 | tf_op jit(solution)/shard_map/ppermute | solution.py:25
  28.0 2.5 %collective-permute-start.1 = (bf16[128,256]{1,0:T(8,128)(2,1)S(1)}, bf16[128,256]{1,0:T(8,128)(2,1)S(1)}, u32[]{:S(2)}, u32[]{:S(2)}) collective-permute-start(bf16[128,256]{1,0:T(8,128)(2,1)S(1)} %get-tuple-element.10), channel_id=1, source_target_pairs={{0,2},{1,3},{2,0},{3,1},{4,6},{5,7},{6,4},{7,5},{8,10},{9,11},{10,... | collective-permute-start | bytes 196616 | tf_op jit(solution)/shard_map/ppermute | solution.py:25
  30.5 6.3 %collective-permute-start.2 = (bf16[128,256]{1,0:T(8,128)(2,1)S(1)}, bf16[128,256]{1,0:T(8,128)(2,1)S(1)}, u32[]{:S(2)}, u32[]{:S(2)}) collective-permute-start(bf16[128,256]{1,0:T(8,128)(2,1)S(1)} %get-tuple-element.9), channel_id=1, source_target_pairs={{0,1},{1,2},{2,3},{3,0},{4,5},{5,6},{6,7},{7,4},{8,9},{9,10},{10,1... | collective-permute-start | bytes 196616 | tf_op jit(solution)/shard_map/ppermute | solution.py:25
  37.0 2.9 %fusion.2 = bf16[512,8,128]{2,1,0:T(8,128)(2,1)S(1)} fusion(s32[512,16,128]{2,1,0:T(8,128)} %param.13, s32[512,16]{1,0:T(8,128)S(1)} %copy.33), kind=kOutput, calls=%fused_computation.3 | convolution fusion | flops 18415616 | bytes 5275648 | tf_op jit(solution)/shard_map/rkn,rkb->rnb/dot_general | solution.py:52
  40.0 0.5 fusion.9
  40.7 2.5 %collective-permute-start.5 = (bf16[128,256]{1,0:T(8,128)(2,1)S(1)}, bf16[128,256]{1,0:T(8,128)(2,1)S(1)}, u32[]{:S(2)}, u32[]{:S(2)}) collective-permute-start(bf16[128,256]{1,0:T(8,128)(2,1)S(1)} %get-tuple-element.15), channel_id=1, source_target_pairs={{0,3},{1,0},{2,1},{3,2},{4,7},{5,4},{6,5},{7,6},{8,11},{9,8},{10,9... | collective-permute-start | bytes 196616 | tf_op jit(solution)/shard_map/ppermute | solution.py:25
  43.3 9.7 %collective-permute-start.6 = (bf16[128,256]{1,0:T(8,128)(2,1)S(1)}, bf16[128,256]{1,0:T(8,128)(2,1)S(1)}, u32[]{:S(2)}, u32[]{:S(2)}) collective-permute-start(bf16[128,256]{1,0:T(8,128)(2,1)S(1)} %get-tuple-element.14), channel_id=1, source_target_pairs={{0,2},{1,3},{2,0},{3,1},{4,6},{5,7},{6,4},{7,5},{8,10},{9,11},{10,... | collective-permute-start | bytes 196616 | tf_op jit(solution)/shard_map/ppermute | solution.py:25
  53.0 1.9 %collective-permute-start.7 = (bf16[128,256]{1,0:T(8,128)(2,1)S(1)}, bf16[128,256]{1,0:T(8,128)(2,1)S(1)}, u32[]{:S(2)}, u32[]{:S(2)}) collective-permute-start(bf16[128,256]{1,0:T(8,128)(2,1)S(1)} %get-tuple-element.13), channel_id=1, source_target_pairs={{0,1},{1,2},{2,3},{3,0},{4,5},{5,6},{6,7},{7,4},{8,9},{9,10},{10,1... | collective-permute-start | bytes 196616 | tf_op jit(solution)/shard_map/ppermute | solution.py:25
  55.4 2.3 %collective-permute-done.6 = bf16[128,256]{1,0:T(8,128)(2,1)S(1)} collective-permute-done((bf16[128,256]{1,0:T(8,128)(2,1)S(1)}, bf16[128,256]{1,0:T(8,128)(2,1)S(1)}, u32[]{:S(2)}, u32[]{:S(2)}) %collective-permute-start.6) | collective-permute-done | bytes 65568 | tf_op jit(solution)/shard_map/ppermute | solution.py:25
  57.7 4.5 %collective-permute-done.7 = bf16[128,256]{1,0:T(8,128)(2,1)S(1)} collective-permute-done((bf16[128,256]{1,0:T(8,128)(2,1)S(1)}, bf16[128,256]{1,0:T(8,128)(2,1)S(1)}, u32[]{:S(2)}, u32[]{:S(2)}) %collective-permute-start.7) | collective-permute-done | bytes 65568 | tf_op jit(solution)/shard_map/ppermute | solution.py:25
  62.2 0.6 fusion.30
  64.5 2.3 %collective-permute-start.8 = (bf16[128,256]{0,1:T(8,128)(2,1)S(1)}, bf16[128,256]{0,1:T(8,128)(2,1)S(1)}, u32[]{:S(2)}, u32[]{:S(2)}) collective-permute-start(bf16[128,256]{0,1:T(8,128)(2,1)S(1)} %get-tuple-element.7), channel_id=1, source_target_pairs={{0,3},{1,0},{2,1},{3,2},{4,7},{5,4},{6,5},{7,6},{8,11},{9,8},{10,9... | collective-permute-start | bytes 196616 | tf_op jit(solution)/shard_map/ppermute | solution.py:25
  66.8 6.7 %collective-permute-start.9 = (bf16[128,256]{0,1:T(8,128)(2,1)S(1)}, bf16[128,256]{0,1:T(8,128)(2,1)S(1)}, u32[]{:S(2)}, u32[]{:S(2)}) collective-permute-start(bf16[128,256]{0,1:T(8,128)(2,1)S(1)} %get-tuple-element.6), channel_id=1, source_target_pairs={{0,2},{1,3},{2,0},{3,1},{4,6},{5,7},{6,4},{7,5},{8,10},{9,11},{10,... | collective-permute-start | bytes 196616 | tf_op jit(solution)/shard_map/ppermute | solution.py:25
  73.5 3.4 %collective-permute-start.10 = (bf16[128,256]{0,1:T(8,128)(2,1)S(1)}, bf16[128,256]{0,1:T(8,128)(2,1)S(1)}, u32[]{:S(2)}, u32[]{:S(2)}) collective-permute-start(bf16[128,256]{0,1:T(8,128)(2,1)S(1)} %get-tuple-element.5), channel_id=1, source_target_pairs={{0,1},{1,2},{2,3},{3,0},{4,5},{5,6},{6,7},{7,4},{8,9},{9,10},{10,1... | collective-permute-start | bytes 196616 | tf_op jit(solution)/shard_map/ppermute | solution.py:25
  77.0 2.4 %collective-permute-done.9 = bf16[128,256]{0,1:T(8,128)(2,1)S(1)} collective-permute-done((bf16[128,256]{0,1:T(8,128)(2,1)S(1)}, bf16[128,256]{0,1:T(8,128)(2,1)S(1)}, u32[]{:S(2)}, u32[]{:S(2)}) %collective-permute-start.9) | collective-permute-done | bytes 65568 | tf_op jit(solution)/shard_map/ppermute | solution.py:25
  79.4 4.2 %collective-permute-done.10 = bf16[128,256]{0,1:T(8,128)(2,1)S(1)} collective-permute-done((bf16[128,256]{0,1:T(8,128)(2,1)S(1)}, bf16[128,256]{0,1:T(8,128)(2,1)S(1)}, u32[]{:S(2)}, u32[]{:S(2)}) %collective-permute-start.10) | collective-permute-done | bytes 65568 | tf_op jit(solution)/shard_map/ppermute | solution.py:25
  84.4 0.7 copy.67
  85.1 0.7 copy.68
  (39 shorter events, 3.4 us)
Async XLA Ops:
  0.6 36.2 %copy-start.2 = (s32[512,16]{0,1:T(8,128)S(1)}, s32[512,16]{0,1:T(8,128)}, u32[]{:S(2)}) copy-start(s32[512,16]{0,1:T(8,128)} %param.14) | copy-start | bytes 98308
  3.4 36.5 %collective-permute-start.3 = (bf16[256,256]{0,1:T(8,128)(2,1)S(1)}, bf16[256,256]{0,1:T(8,128)(2,1)S(1)}, u32[]{:S(2)}, u32[]{:S(2)}) collective-permute-start(bf16[256,256]{0,1:T(8,128)(2,1)S(1)} %get-tuple-element.17), channel_id=1, source_target_pairs={{0,4},{4,8},{8,12},{12,16},{16,20},{20,24},{24,28},{28,32},{32,36}... | collective-permute-start | bytes 393224 | tf_op jit(solution)/shard_map/ppermute | solution.py:12
  5.4 34.6 %collective-permute-start.4 = (bf16[256,256]{0,1:T(8,128)(2,1)S(1)}, bf16[256,256]{0,1:T(8,128)(2,1)S(1)}, u32[]{:S(2)}, u32[]{:S(2)}) collective-permute-start(bf16[256,256]{0,1:T(8,128)(2,1)S(1)} %get-tuple-element.18), channel_id=1, source_target_pairs={{4,0},{8,4},{12,8},{16,12},{20,16},{24,20},{28,24},{32,28},{36,32}... | collective-permute-start | bytes 393224 | tf_op jit(solution)/shard_map/ppermute | solution.py:12
  13.4 39.5 %collective-permute-start = (bf16[128,256]{1,0:T(8,128)(2,1)S(1)}, bf16[128,256]{1,0:T(8,128)(2,1)S(1)}, u32[]{:S(2)}, u32[]{:S(2)}) collective-permute-start(bf16[128,256]{1,0:T(8,128)(2,1)S(1)} %get-tuple-element.11), channel_id=1, source_target_pairs={{0,3},{1,0},{2,1},{3,2},{4,7},{5,4},{6,5},{7,6},{8,11},{9,8},{10,9... | collective-permute-start | bytes 196616 | tf_op jit(solution)/shard_map/ppermute | solution.py:25
  28.0 27.3 %collective-permute-start.1 = (bf16[128,256]{1,0:T(8,128)(2,1)S(1)}, bf16[128,256]{1,0:T(8,128)(2,1)S(1)}, u32[]{:S(2)}, u32[]{:S(2)}) collective-permute-start(bf16[128,256]{1,0:T(8,128)(2,1)S(1)} %get-tuple-element.10), channel_id=1, source_target_pairs={{0,2},{1,3},{2,0},{3,1},{4,6},{5,7},{6,4},{7,5},{8,10},{9,11},{10,... | collective-permute-start | bytes 196616 | tf_op jit(solution)/shard_map/ppermute | solution.py:25
  30.5 24.9 %collective-permute-start.2 = (bf16[128,256]{1,0:T(8,128)(2,1)S(1)}, bf16[128,256]{1,0:T(8,128)(2,1)S(1)}, u32[]{:S(2)}, u32[]{:S(2)}) collective-permute-start(bf16[128,256]{1,0:T(8,128)(2,1)S(1)} %get-tuple-element.9), channel_id=1, source_target_pairs={{0,1},{1,2},{2,3},{3,0},{4,5},{5,6},{6,7},{7,4},{8,9},{9,10},{10,1... | collective-permute-start | bytes 196616 | tf_op jit(solution)/shard_map/ppermute | solution.py:25
  40.0 14.9 %copy-start = (bf16[512,512]{1,0:T(8,128)(2,1)S(1)}, bf16[512,512]{1,0:T(8,128)(2,1)}, u32[]{:S(2)}) copy-start(bf16[512,512]{1,0:T(8,128)(2,1)} %param.12) | copy-start | bytes 1572868
  40.5 14.7 %copy-start.1 = (bf16[512,512]{1,0:T(8,128)(2,1)S(1)}, bf16[512,512]{1,0:T(8,128)(2,1)}, u32[]{:S(2)}) copy-start(bf16[512,512]{1,0:T(8,128)(2,1)} %param.11) | copy-start | bytes 1572868
  40.7 14.6 %collective-permute-start.5 = (bf16[128,256]{1,0:T(8,128)(2,1)S(1)}, bf16[128,256]{1,0:T(8,128)(2,1)S(1)}, u32[]{:S(2)}, u32[]{:S(2)}) collective-permute-start(bf16[128,256]{1,0:T(8,128)(2,1)S(1)} %get-tuple-element.15), channel_id=1, source_target_pairs={{0,3},{1,0},{2,1},{3,2},{4,7},{5,4},{6,5},{7,6},{8,11},{9,8},{10,9... | collective-permute-start | bytes 196616 | tf_op jit(solution)/shard_map/ppermute | solution.py:25
  43.3 14.4 %collective-permute-start.6 = (bf16[128,256]{1,0:T(8,128)(2,1)S(1)}, bf16[128,256]{1,0:T(8,128)(2,1)S(1)}, u32[]{:S(2)}, u32[]{:S(2)}) collective-permute-start(bf16[128,256]{1,0:T(8,128)(2,1)S(1)} %get-tuple-element.14), channel_id=1, source_target_pairs={{0,2},{1,3},{2,0},{3,1},{4,6},{5,7},{6,4},{7,5},{8,10},{9,11},{10,... | collective-permute-start | bytes 196616 | tf_op jit(solution)/shard_map/ppermute | solution.py:25
  53.0 9.2 %collective-permute-start.7 = (bf16[128,256]{1,0:T(8,128)(2,1)S(1)}, bf16[128,256]{1,0:T(8,128)(2,1)S(1)}, u32[]{:S(2)}, u32[]{:S(2)}) collective-permute-start(bf16[128,256]{1,0:T(8,128)(2,1)S(1)} %get-tuple-element.13), channel_id=1, source_target_pairs={{0,1},{1,2},{2,3},{3,0},{4,5},{5,6},{6,7},{7,4},{8,9},{9,10},{10,1... | collective-permute-start | bytes 196616 | tf_op jit(solution)/shard_map/ppermute | solution.py:25
  64.5 12.4 %collective-permute-start.8 = (bf16[128,256]{0,1:T(8,128)(2,1)S(1)}, bf16[128,256]{0,1:T(8,128)(2,1)S(1)}, u32[]{:S(2)}, u32[]{:S(2)}) collective-permute-start(bf16[128,256]{0,1:T(8,128)(2,1)S(1)} %get-tuple-element.7), channel_id=1, source_target_pairs={{0,3},{1,0},{2,1},{3,2},{4,7},{5,4},{6,5},{7,6},{8,11},{9,8},{10,9... | collective-permute-start | bytes 196616 | tf_op jit(solution)/shard_map/ppermute | solution.py:25
  66.8 12.6 %collective-permute-start.9 = (bf16[128,256]{0,1:T(8,128)(2,1)S(1)}, bf16[128,256]{0,1:T(8,128)(2,1)S(1)}, u32[]{:S(2)}, u32[]{:S(2)}) collective-permute-start(bf16[128,256]{0,1:T(8,128)(2,1)S(1)} %get-tuple-element.6), channel_id=1, source_target_pairs={{0,2},{1,3},{2,0},{3,1},{4,6},{5,7},{6,4},{7,5},{8,10},{9,11},{10,... | collective-permute-start | bytes 196616 | tf_op jit(solution)/shard_map/ppermute | solution.py:25
  73.5 10.0 %collective-permute-start.10 = (bf16[128,256]{0,1:T(8,128)(2,1)S(1)}, bf16[128,256]{0,1:T(8,128)(2,1)S(1)}, u32[]{:S(2)}, u32[]{:S(2)}) collective-permute-start(bf16[128,256]{0,1:T(8,128)(2,1)S(1)} %get-tuple-element.5), channel_id=1, source_target_pairs={{0,1},{1,2},{2,3},{3,0},{4,5},{5,6},{6,7},{7,4},{8,9},{9,10},{10,1... | collective-permute-start | bytes 196616 | tf_op jit(solution)/shard_map/ppermute | solution.py:25

commit v3 on v2

--- a/solution.py
+++ b/solution.py
@@ -3,7 +3,7 @@
 from jax import lax
 from jax.sharding import PartitionSpec as P
 
-USE_ALL_TO_ALL = False
+USE_ALL_TO_ALL = True
 
 
 def shifted(block, axis, distance):
@@ -36,8 +36,6 @@
     inverse = 1.0 / degree.astype(jnp.float32)
     scaled = (out_grad.astype(jnp.float32) * inverse[:, None]).astype(jnp.bfloat16)
 
-    own_in = swap_chunks(jnp.concatenate([features, out_grad], axis=1), "col")
-
     reach = 2 * block
     pair = jnp.concatenate([features, scaled], axis=1)
     from_prev = shifted(pair[rows_here - reach:], "row", 1)
@@ -56,10 +54,11 @@
     sums = jnp.dot(slab, window, preferred_element_type=jnp.float32)
     aggregated = (sums[:, :part] * inverse[:, None]).astype(jnp.bfloat16)
     back_agg = sums[:, part:].astype(jnp.bfloat16)
-    agg_in = swap_chunks(jnp.concatenate([aggregated, back_agg], axis=1), "col")
-
-    own_in = own_in.reshape(n_col, chunk, 2, part)
-    agg_in = agg_in.reshape(n_col, chunk, 2, part)
+    ins = swap_chunks(
+        jnp.concatenate([features, out_grad, aggregated, back_agg], axis=1), "col"
+    ).reshape(n_col, chunk, 4, part)
+    own_in = ins[:, :, :2]
+    agg_in = ins[:, :, 2:]
     ws = self_weight.reshape(n_col, part, width)
     wn = neigh_weight.reshape(n_col, part, width)
     ws_t = self_weight.T.reshape(n_col, part, width)

time: 86.3 us -> 76 us (0.88)
  the two profiles are of different devices: /device:TPU:32 before, /device:TPU:102 now
where the time goes in v3:
time: 76 us; the launch traced here: 75.6 us
  waiting for transfers between devices  24.7 us (32%)
  blocking collectives  19.9 us (26%)
  starting transfers between devices  19.2 us (25%)
  matrix products  4.42 us (6%)
  local copies, waits for them, and re-layouts  4.14 us (5%)
  other arithmetic  2.44 us (3%)
  between operations  0.83 us (1%)
    all_to_all x1, waiting for transfers between devices, swap_chunks(): return lax.all_to_all(block, axis, 0, 0, tiled=True)  24.7 us
    all_to_all x1, blocking collectives, swap_chunks(): return lax.all_to_all(block, axis, 0, 0, tiled=True)  19.9 us
    all_to_all x1, starting transfers between devices, swap_chunks(): return lax.all_to_all(block, axis, 0, 0, tiled=True)  13.6 us
    ppermute x2, starting transfers between devices, shifted(): return lax.ppermute(block, axis, route)  5.56 us
    dot_general x1, matrix products, per_device(): jnp.einsum('rkn,rkb->rnb', owner, tile_rows.astype(jnp.bfloat16), preferr...  2.94 us
    unnamed x7, local copies, waits for them, and re-layouts  2.76 us
  transfers between devices with their start and end apart: 3, of which 1 were waited for; matrix products, arithmetic and copies ran while one was open for 6% of the time, Pallas kernels for 0%

profile of v3, /device:TPU:102, one launch (start us, length us, event | category | flops | bytes accessed | tf_op | source)
XLA Modules:
  0.0 75.6 jit_solution(17978202580258117558)
XLA Ops:
  0.6 1.0 %copy.35 = bf16[512,128]{0,1:T(8,128)(2,1)S(1)} copy(bf16[512,128]{1,0:T(8,128)(2,1)} %param.8) | data formatting | bytes 262144 | tf_op args[1]
  1.6 0.7 convert_divide_fusion
  2.3 1.0 %copy.34 = bf16[512,128]{0,1:T(8,128)(2,1)S(1)} copy(bf16[512,128]{1,0:T(8,128)(2,1)} %param.7) | data formatting | bytes 262144 | tf_op args[0]
  3.4 1.9 %collective-permute-start = (bf16[256,256]{0,1:T(8,128)(2,1)S(1)}, bf16[256,256]{0,1:T(8,128)(2,1)S(1)}, u32[]{:S(2)}, u32[]{:S(2)}) collective-permute-start(bf16[256,256]{0,1:T(8,128)(2,1)S(1)} %get-tuple-element.4), channel_id=1, source_target_pairs={{0,4},{4,8},{8,12},{12,16},{16,20},{20,24},{24,28},{28,32},{32,36}... | collective-permute-start | bytes 393224 | tf_op jit(solution)/shard_map/ppermute | solution.py:12
  5.3 3.6 %collective-permute-start.1 = (bf16[256,256]{0,1:T(8,128)(2,1)S(1)}, bf16[256,256]{0,1:T(8,128)(2,1)S(1)}, u32[]{:S(2)}, u32[]{:S(2)}) collective-permute-start(bf16[256,256]{0,1:T(8,128)(2,1)S(1)} %get-tuple-element.5), channel_id=1, source_target_pairs={{4,0},{8,4},{12,8},{16,12},{20,16},{24,20},{28,24},{32,28},{36,32}... | collective-permute-start | bytes 393224 | tf_op jit(solution)/shard_map/ppermute | solution.py:12
  9.0 0.8 %broadcast_subtract_fusion = s32[512,16]{0,1:T(8,128)S(1)} fusion(s32[512,16]{0,1:T(8,128)} %param.12, s32[]{:T(128)S(6)} %sub.9), kind=kLoop, calls=%fused_computation.40 | loop fusion | flops 8192 | bytes 65540 | tf_op jit(solution)/shard_map/sub | solution.py:46
  9.8 0.1 copy.31
  9.9 2.9 %fusion.2 = bf16[512,8,128]{2,1,0:T(8,128)(2,1)S(1)} fusion(s32[512,16,128]{2,1,0:T(8,128)} %param.11, s32[512,16]{1,0:T(8,128)S(1)} %copy.31), kind=kOutput, calls=%fused_computation.3 | convolution fusion | flops 18415616 | bytes 5275648 | tf_op jit(solution)/shard_map/rkn,rkb->rnb/dot_general | solution.py:50
  12.9 0.5 fusion.9
  13.4 0.9 %copy_bitcast_fusion = bf16[4,128,512]{1,2,0:T(8,128)(2,1)} fusion(bf16[512,128]{0,1:T(8,128)(2,1)S(1)} %slice.75, bf16[512,128]{0,1:T(8,128)(2,1)S(1)} %fusion.20, bf16[512,128]{0,1:T(8,128)(2,1)S(1)} %copy.35, bf16[512,128]{0,1:T(8,128)(2,1)S(1)} %copy.34), kind=kLoop, calls=%fused_computation.16 | loop fusion | flops 2097152 | bytes 1048576 | tf_op jit(solution)/shard_map/all_to_all | solution.py:18
  14.3 13.6 %all-to-all-start = ((bf16[4,128,512]{1,2,0:T(8,128)(2,1)}), bf16[4,128,512]{1,2,0:T(8,128)(2,1)S(1)}, u32[]{:S(2)}, u32[]{:S(2)}) async-start(bf16[4,128,512]{1,2,0:T(8,128)(2,1)} %copy_bitcast_fusion), calls=%async_computation | async-start | bytes 1048576 | tf_op jit(solution)/shard_map/all_to_all | solution.py:18
  27.9 0.2 copy.48
  28.1 0.2 copy.47
  28.4 24.7 %all-to-all-done = bf16[4,128,512]{1,2,0:T(8,128)(2,1)S(1)} async-done(((bf16[4,128,512]{1,2,0:T(8,128)(2,1)}), bf16[4,128,512]{1,2,0:T(8,128)(2,1)S(1)}, u32[]{:S(2)}, u32[]{:S(2)}) %all-to-all-start) | async-done | bytes 524320 | tf_op jit(solution)/shard_map/all_to_all | solution.py:18
  53.1 0.2 convolution_bitcast_fusion.2
  53.3 0.3 fusion.8
  53.6 0.1 copy.46
  53.7 0.3 convolution_bitcast_fusion
  54.0 0.3 fusion.7
  54.2 0.1 copy.49
  54.4 19.9 %all_to_all.18 = bf16[4,128,256]{1,2,0:T(8,128)(2,1)S(1)} all-to-all(bf16[4,128,256]{1,2,0:T(8,128)(2,1)S(1)} %bitcast.71), channel_id=1, replica_groups=mesh['row'=192,'col'=4] {'col'}, dimensions={0} | all-to-all | bytes 524288 | tf_op jit(solution)/shard_map/all_to_all | solution.py:18
  74.3 0.1 copy.45
  74.5 0.4 fusion.23
  74.9 0.7 copy_bitcast_fusion.1
  (12 shorter events, 0.2 us)
Async XLA Ops:
  3.4 9.4 %collective-permute-start = (bf16[256,256]{0,1:T(8,128)(2,1)S(1)}, bf16[256,256]{0,1:T(8,128)(2,1)S(1)}, u32[]{:S(2)}, u32[]{:S(2)}) collective-permute-start(bf16[256,256]{0,1:T(8,128)(2,1)S(1)} %get-tuple-element.4), channel_id=1, source_target_pairs={{0,4},{4,8},{8,12},{12,16},{16,20},{20,24},{24,28},{28,32},{32,36}... | collective-permute-start | bytes 393224 | tf_op jit(solution)/shard_map/ppermute | solution.py:12
  5.3 7.5 %collective-permute-start.1 = (bf16[256,256]{0,1:T(8,128)(2,1)S(1)}, bf16[256,256]{0,1:T(8,128)(2,1)S(1)}, u32[]{:S(2)}, u32[]{:S(2)}) collective-permute-start(bf16[256,256]{0,1:T(8,128)(2,1)S(1)} %get-tuple-element.5), channel_id=1, source_target_pairs={{4,0},{8,4},{12,8},{16,12},{20,16},{24,20},{28,24},{32,28},{36,32}... | collective-permute-start | bytes 393224 | tf_op jit(solution)/shard_map/ppermute | solution.py:12
  13.3 14.6 %copy-start = (bf16[512,512]{1,0:T(8,128)(2,1)S(1)}, bf16[512,512]{1,0:T(8,128)(2,1)}, u32[]{:S(2)}) copy-start(bf16[512,512]{1,0:T(8,128)(2,1)} %param.10) | copy-start | bytes 1572868
  13.4 14.8 %copy-start.1 = (bf16[512,512]{1,0:T(8,128)(2,1)S(1)}, bf16[512,512]{1,0:T(8,128)(2,1)}, u32[]{:S(2)}) copy-start(bf16[512,512]{1,0:T(8,128)(2,1)} %param.9) | copy-start | bytes 1572868
  14.3 38.8 %all-to-all-start = ((bf16[4,128,512]{1,2,0:T(8,128)(2,1)}), bf16[4,128,512]{1,2,0:T(8,128)(2,1)S(1)}, u32[]{:S(2)}, u32[]{:S(2)}) async-start(bf16[4,128,512]{1,2,0:T(8,128)(2,1)} %copy_bitcast_fusion), calls=%async_computation | async-start | bytes 1048576 | tf_op jit(solution)/shard_map/all_to_all | solution.py:18

commit v4 on v3

--- a/solution.py
+++ b/solution.py
@@ -43,13 +43,13 @@
     window = jnp.concatenate([from_prev, pair, from_next], axis=0)
     window_blocks = window.shape[0] // block
     first_block = lax.axis_index("row") * (rows_here // block) - reach // block
-    local_cols = tile_cols - first_block
+    blocks_here = rows_here // block
+    local_cols = tile_cols.reshape(blocks_here, block, -1)[:, 0] - first_block
     owner = (
         local_cols[:, :, None] == jnp.arange(window_blocks, dtype=jnp.int32)[None, None, :]
     ).astype(jnp.bfloat16)
-    slab = jnp.einsum(
-        "rkn,rkb->rnb", owner, tile_rows.astype(jnp.bfloat16), preferred_element_type=jnp.float32
-    )
+    tiles = tile_rows.astype(jnp.bfloat16).reshape(blocks_here, block, -1, block)
+    slab = jnp.einsum("akn,arkb->arnb", owner, tiles, preferred_element_type=jnp.float32)
     slab = slab.astype(jnp.bfloat16).reshape(rows_here, window_blocks * block)
     sums = jnp.dot(slab, window, preferred_element_type=jnp.float32)
     aggregated = (sums[:, :part] * inverse[:, None]).astype(jnp.bfloat16)

time: 76 us -> 73.3 us (0.964)
  the two profiles are of different devices: /device:TPU:102 before, /device:TPU:111 now
where the time goes in v4:
time: 73.3 us; the launch traced here: 73 us
  waiting for transfers between devices  22.9 us (31%)
  starting transfers between devices  21 us (29%)
  blocking collectives  18.1 us (25%)
  other arithmetic  4.15 us (6%)
  local copies, waits for them, and re-layouts  4.14 us (6%)
  matrix products  1.92 us (3%)
  between operations  0.84 us (1%)
    all_to_all x1, waiting for transfers between devices, swap_chunks(): return lax.all_to_all(block, axis, 0, 0, tiled=True)  22.9 us
    all_to_all x1, blocking collectives, swap_chunks(): return lax.all_to_all(block, axis, 0, 0, tiled=True)  18.1 us
    all_to_all x1, starting transfers between devices, swap_chunks(): return lax.all_to_all(block, axis, 0, 0, tiled=True)  13.3 us
    ppermute x2, starting transfers between devices, shifted(): return lax.ppermute(block, axis, route)  7.67 us
    unnamed x10, local copies, waits for them, and re-layouts  2.87 us
    convert_element_type x1, other arithmetic, per_device(): tile_rows.astype(jnp.bfloat16).reshape(blocks_here, block, -1, block)  2.47 us
  transfers between devices with their start and end apart: 3, of which 1 were waited for; matrix products, arithmetic and copies ran while one was open for 5% of the time, Pallas kernels for 0%

profile of v4, /device:TPU:111, one launch (start us, length us, event | category | flops | bytes accessed | tf_op | source)
XLA Modules:
  0.0 73.0 jit_solution(16112252316753703232)
XLA Ops:
  0.6 1.0 %copy.34 = bf16[512,128]{0,1:T(8,128)(2,1)S(1)} copy(bf16[512,128]{1,0:T(8,128)(2,1)} %param.7) | data formatting | bytes 262144 | tf_op args[0]
  1.6 1.0 %copy.35 = bf16[512,128]{0,1:T(8,128)(2,1)S(1)} copy(bf16[512,128]{1,0:T(8,128)(2,1)} %param.8) | data formatting | bytes 262144 | tf_op args[1]
  2.7 0.7 convert_divide_fusion
  3.4 2.6 %collective-permute-start.1 = (bf16[256,256]{0,1:T(8,128)(2,1)S(1)}, bf16[256,256]{0,1:T(8,128)(2,1)S(1)}, u32[]{:S(2)}, u32[]{:S(2)}) collective-permute-start(bf16[256,256]{0,1:T(8,128)(2,1)S(1)} %get-tuple-element.5), channel_id=1, source_target_pairs={{4,0},{8,4},{12,8},{16,12},{20,16},{24,20},{28,24},{32,28},{36,32}... | collective-permute-start | bytes 393224 | tf_op jit(solution)/shard_map/ppermute | solution.py:12
  6.0 5.1 %collective-permute-start = (bf16[256,256]{0,1:T(8,128)(2,1)S(1)}, bf16[256,256]{0,1:T(8,128)(2,1)S(1)}, u32[]{:S(2)}, u32[]{:S(2)}) collective-permute-start(bf16[256,256]{0,1:T(8,128)(2,1)S(1)} %get-tuple-element.4), channel_id=1, source_target_pairs={{0,4},{4,8},{8,12},{12,16},{16,20},{20,24},{24,28},{28,32},{32,36}... | collective-permute-start | bytes 393224 | tf_op jit(solution)/shard_map/ppermute | solution.py:12
  11.1 2.5 %convert_element_type.29 = bf16[512,16,128]{2,1,0:T(8,128)(2,1)S(1)} convert(s32[512,16,128]{2,1,0:T(8,128)} %param.11) | non-fusion elementwise | flops 1048576 | bytes 6291456 | tf_op jit(solution)/shard_map/convert_element_type | solution.py:51
  13.6 0.1 copy.53
  13.7 0.4 convolution_convert_fusion
  14.2 0.5 fusion.4
  14.7 0.9 %copy_bitcast_fusion = bf16[4,128,512]{1,2,0:T(8,128)(2,1)} fusion(bf16[512,128]{0,1:T(8,128)(2,1)S(1)} %slice.80, bf16[512,128]{0,1:T(8,128)(2,1)S(1)} %fusion.14, bf16[512,128]{0,1:T(8,128)(2,1)S(1)} %copy.35, bf16[512,128]{0,1:T(8,128)(2,1)S(1)} %copy.34), kind=kLoop, calls=%fused_computation.12 | loop fusion | flops 2097152 | bytes 1048576 | tf_op jit(solution)/shard_map/all_to_all | solution.py:18
  15.6 13.3 %all-to-all-start = ((bf16[4,128,512]{1,2,0:T(8,128)(2,1)}), bf16[4,128,512]{1,2,0:T(8,128)(2,1)S(1)}, u32[]{:S(2)}, u32[]{:S(2)}) async-start(bf16[4,128,512]{1,2,0:T(8,128)(2,1)} %copy_bitcast_fusion), calls=%async_computation | async-start | bytes 1048576 | tf_op jit(solution)/shard_map/all_to_all | solution.py:18
  29.0 0.2 copy.49
  29.2 0.2 copy.48
  29.4 22.9 %all-to-all-done = bf16[4,128,512]{1,2,0:T(8,128)(2,1)S(1)} async-done(((bf16[4,128,512]{1,2,0:T(8,128)(2,1)}), bf16[4,128,512]{1,2,0:T(8,128)(2,1)S(1)}, u32[]{:S(2)}, u32[]{:S(2)}) %all-to-all-start) | async-done | bytes 524320 | tf_op jit(solution)/shard_map/all_to_all | solution.py:18
  52.3 0.2 convolution_bitcast_fusion
  52.5 0.3 fusion.2
  52.8 0.1 copy.50
  52.9 0.3 convolution_bitcast_fusion.2
  53.2 0.3 fusion.3
  53.4 0.1 copy.47
  53.6 18.1 %all_to_all.18 = bf16[4,128,256]{1,2,0:T(8,128)(2,1)S(1)} all-to-all(bf16[4,128,256]{1,2,0:T(8,128)(2,1)S(1)} %bitcast.86), channel_id=1, replica_groups=mesh['row'=192,'col'=4] {'col'}, dimensions={0} | all-to-all | bytes 524288 | tf_op jit(solution)/shard_map/all_to_all | solution.py:18
  71.7 0.1 copy.45
  71.9 0.4 fusion.20
  72.3 0.7 %copy_bitcast_fusion.1 = (bf16[512,128]{1,0:T(8,128)(2,1)}, bf16[512,128]{1,0:T(8,128)(2,1)}) fusion(bf16[512,1,128]{2,1,0:T(2,128)(2,1)S(1)} %get-tuple-element.2, bf16[512,1,128]{2,1,0:T(2,128)(2,1)S(1)} %get-tuple-element.3), kind=kLoop, calls=%fused_computation.34 | loop fusion | bytes 524288
  (16 shorter events, 0.2 us)
Async XLA Ops:
  3.4 10.7 %collective-permute-start.1 = (bf16[256,256]{0,1:T(8,128)(2,1)S(1)}, bf16[256,256]{0,1:T(8,128)(2,1)S(1)}, u32[]{:S(2)}, u32[]{:S(2)}) collective-permute-start(bf16[256,256]{0,1:T(8,128)(2,1)S(1)} %get-tuple-element.5), channel_id=1, source_target_pairs={{4,0},{8,4},{12,8},{16,12},{20,16},{24,20},{28,24},{32,28},{36,32}... | collective-permute-start | bytes 393224 | tf_op jit(solution)/shard_map/ppermute | solution.py:12
  6.0 8.2 %collective-permute-start = (bf16[256,256]{0,1:T(8,128)(2,1)S(1)}, bf16[256,256]{0,1:T(8,128)(2,1)S(1)}, u32[]{:S(2)}, u32[]{:S(2)}) collective-permute-start(bf16[256,256]{0,1:T(8,128)(2,1)S(1)} %get-tuple-element.4), channel_id=1, source_target_pairs={{0,4},{4,8},{8,12},{12,16},{16,20},{20,24},{24,28},{28,32},{32,36}... | collective-permute-start | bytes 393224 | tf_op jit(solution)/shard_map/ppermute | solution.py:12
  11.1 2.5 %copy-start.2 = (s32[512,16]{0,1:T(8,128)S(1)}, s32[512,16]{0,1:T(8,128)}, u32[]{:S(2)}) copy-start(s32[512,16]{0,1:T(8,128)} %param.12) | copy-start | bytes 98308
  14.7 14.3 %copy-start = (bf16[512,512]{1,0:T(8,128)(2,1)S(1)}, bf16[512,512]{1,0:T(8,128)(2,1)}, u32[]{:S(2)}) copy-start(bf16[512,512]{1,0:T(8,128)(2,1)} %param.10) | copy-start | bytes 1572868
  14.7 14.5 %copy-start.1 = (bf16[512,512]{1,0:T(8,128)(2,1)S(1)}, bf16[512,512]{1,0:T(8,128)(2,1)}, u32[]{:S(2)}) copy-start(bf16[512,512]{1,0:T(8,128)(2,1)} %param.9) | copy-start | bytes 1572868
  15.6 36.6 %all-to-all-start = ((bf16[4,128,512]{1,2,0:T(8,128)(2,1)}), bf16[4,128,512]{1,2,0:T(8,128)(2,1)S(1)}, u32[]{:S(2)}, u32[]{:S(2)}) async-start(bf16[4,128,512]{1,2,0:T(8,128)(2,1)} %copy_bitcast_fusion), calls=%async_computation | async-start | bytes 1048576 | tf_op jit(solution)/shard_map/all_to_all | solution.py:18

commit v5 on v4

--- a/solution.py
+++ b/solution.py
@@ -2,6 +2,11 @@
 import jax.numpy as jnp
 from jax import lax
 from jax.sharding import PartitionSpec as P
+from jax.experimental import pallas as pl
+from jax.experimental.pallas import tpu as pltpu
+import os
+
+INTERPRET = bool(os.environ.get("SOL_INTERPRET"))
 
 USE_ALL_TO_ALL = True
 
@@ -27,6 +32,35 @@
     return jnp.roll(stacked, me, axis=0).reshape(block.shape)
 
 
+def neighbour_sums(local_cols, rows, window, block):
+    n_rows, slots, _ = rows.shape
+    width = window.shape[1]
+
+    def kernel(cols_ref, rows_ref, win_ref, out_ref):
+        a = pl.program_id(0)
+        acc = jnp.zeros((block, width), jnp.float32)
+        for k in range(slots):
+            start = pl.multiple_of(cols_ref[a * slots + k] * block, block)
+            tile = rows_ref[:, k, :].astype(jnp.float32).astype(jnp.bfloat16)
+            acc += jnp.dot(tile, win_ref[pl.ds(start, block), :], preferred_element_type=jnp.float32)
+        out_ref[...] = acc
+
+    return pl.pallas_call(
+        kernel,
+        out_shape=jax.ShapeDtypeStruct((n_rows, width), jnp.float32),
+        grid_spec=pltpu.PrefetchScalarGridSpec(
+            num_scalar_prefetch=1,
+            grid=(n_rows // block,),
+            in_specs=[
+                pl.BlockSpec((block, slots, block), lambda a, c: (a, 0, 0)),
+                pl.BlockSpec(window.shape, lambda a, c: (0, 0)),
+            ],
+            out_specs=pl.BlockSpec((block, width), lambda a, c: (a, 0)),
+        ),
+        interpret=INTERPRET,
+    )(local_cols, rows, window)
+
+
 def per_device(features, out_grad, self_weight, neigh_weight, tile_rows, tile_cols, degree):
     rows_here, part = features.shape
     block = tile_rows.shape[2]
@@ -45,13 +79,8 @@
     first_block = lax.axis_index("row") * (rows_here // block) - reach // block
     blocks_here = rows_here // block
     local_cols = tile_cols.reshape(blocks_here, block, -1)[:, 0] - first_block
-    owner = (
-        local_cols[:, :, None] == jnp.arange(window_blocks, dtype=jnp.int32)[None, None, :]
-    ).astype(jnp.bfloat16)
-    tiles = tile_rows.astype(jnp.bfloat16).reshape(blocks_here, block, -1, block)
-    slab = jnp.einsum("akn,arkb->arnb", owner, tiles, preferred_element_type=jnp.float32)
-    slab = slab.astype(jnp.bfloat16).reshape(rows_here, window_blocks * block)
-    sums = jnp.dot(slab, window, preferred_element_type=jnp.float32)
+    local_cols = jnp.clip(local_cols, 0, window_blocks - 1).reshape(-1)
+    sums = neighbour_sums(local_cols, tile_rows, window, block)
     aggregated = (sums[:, :part] * inverse[:, None]).astype(jnp.bfloat16)
     back_agg = sums[:, part:].astype(jnp.bfloat16)
     ins = swap_chunks(

time: 73.3 us -> 85.9 us (1.17)
  the two profiles are of different devices: /device:TPU:111 before, /device:TPU:12 now
where the time goes in v5:
time: 85.9 us; the launch traced here: 85.4 us
  waiting for transfers between devices  24.1 us (28%)
  starting transfers between devices  20.1 us (23%)
  blocking collectives  19.9 us (23%)
  Pallas kernels  8.52 us (10%)
  other arithmetic  5.61 us (7%)
  local copies, waits for them, and re-layouts  5.43 us (6%)
  matrix products  1.01 us (1%)
    all_to_all x1, waiting for transfers between devices, swap_chunks(): return lax.all_to_all(block, axis, 0, 0, tiled=True)  23.1 us
    all_to_all x1, blocking collectives, swap_chunks(): return lax.all_to_all(block, axis, 0, 0, tiled=True)  19.9 us
    all_to_all x1, starting transfers between devices, swap_chunks(): return lax.all_to_all(block, axis, 0, 0, tiled=True)  14.5 us
    pallas_call x1, Pallas kernels, neighbour_sums(): pl.pallas_call(kernel, out_shape=jax.ShapeDtypeStruct((n_rows, width), jn...  8.52 us
    ppermute x2, starting transfers between devices, shifted(): return lax.ppermute(block, axis, route)  5.56 us
    concatenate x1, other arithmetic, per_device(): window = jnp.concatenate([from_prev, pair, from_next], axis=0)  1.74 us
  transfers between devices with their start and end apart: 3, of which 2 were waited for; matrix products, arithmetic and copies ran while one was open for 2% of the time, Pallas kernels for 0%

profile of v5, /device:TPU:12, one launch (start us, length us, event | category | flops | bytes accessed | tf_op | source)
XLA Modules:
  0.0 85.4 jit_solution(12490143096382280048)
XLA Ops:
  0.7 0.7 convert_divide_fusion
  1.4 1.0 %multiply_convert_fusion = bf16[512,128]{1,0:T(8,128)(2,1)S(1)} fusion(bf16[512,128]{1,0:T(8,128)(2,1)} %param.8, f32[512]{0:T(512)S(1)} %convert_divide_fusion), kind=kLoop, calls=%fused_computation.16 | loop fusion | flops 196608 | bytes 264192 | tf_op jit(solution)/shard_map/convert_element_type | solution.py:71
  2.4 0.9 %fusion.5 = (bf16[256,256]{1,0:T(8,128)(2,1)S(1)}, bf16[256,256]{1,0:T(8,128)(2,1)S(1)}) fusion(bf16[512,128]{1,0:T(8,128)(2,1)} %param.7, bf16[512,128]{1,0:T(8,128)(2,1)S(1)} %multiply_convert_fusion), kind=kLoop, calls=%fused_computation.17 | loop fusion | flops 524288 | bytes 524288 | tf_op jit(solution)/shard_map/concatenate | solution.py:74
  3.3 1.9 %collective-permute-start = (bf16[256,256]{1,0:T(8,128)(2,1)S(1)}, bf16[256,256]{1,0:T(8,128)(2,1)S(1)}, u32[]{:S(2)}, u32[]{:S(2)}) collective-permute-start(bf16[256,256]{1,0:T(8,128)(2,1)S(1)} %get-tuple-element.4), channel_id=1, source_target_pairs={{0,4},{4,8},{8,12},{12,16},{16,20},{20,24},{24,28},{28,32},{32,36}... | collective-permute-start | bytes 393224 | tf_op jit(solution)/shard_map/ppermute | solution.py:17
  5.3 3.6 %collective-permute-start.1 = (bf16[256,256]{1,0:T(8,128)(2,1)S(1)}, bf16[256,256]{1,0:T(8,128)(2,1)S(1)}, u32[]{:S(2)}, u32[]{:S(2)}) collective-permute-start(bf16[256,256]{1,0:T(8,128)(2,1)S(1)} %get-tuple-element.5), channel_id=1, source_target_pairs={{4,0},{8,4},{12,8},{16,12},{20,16},{24,20},{28,24},{32,28},{36,32}... | collective-permute-start | bytes 393224 | tf_op jit(solution)/shard_map/ppermute | solution.py:17
  8.9 0.8 reshape.46
  9.8 0.6 min.12.cols_ref
  10.4 1.0 %collective-permute-done.1 = bf16[256,256]{1,0:T(8,128)(2,1)S(1)} collective-permute-done((bf16[256,256]{1,0:T(8,128)(2,1)S(1)}, bf16[256,256]{1,0:T(8,128)(2,1)S(1)}, u32[]{:S(2)}, u32[]{:S(2)}) %collective-permute-start.1) | collective-permute-done | bytes 131104 | tf_op jit(solution)/shard_map/ppermute | solution.py:17
  11.4 1.7 %pad_maximum_fusion.win_ref = bf16[1024,256]{1,0:T(8,128)(2,1)} fusion(bf16[256,256]{1,0:T(8,128)(2,1)S(1)} %collective-permute-done.1, bf16[512,128]{1,0:T(8,128)(2,1)S(1)} %multiply_convert_fusion, bf16[512,128]{1,0:T(8,128)(2,1)} %param.7, bf16[256,256]{1,0:T(8,128)(2,1)S(1)} %collective-permute-done), kind=kLoop, calls=%fused_computation.8 | loop fusion | flops 2097152 | bytes 1048576 | tf_op jit(solution)/shard_map/concatenate | solution.py:77
  13.2 8.5 %shard_map.86 = f32[512,256]{1,0:T(8,128)} custom-call(s32[64]{0:T(128)} %min.12.cols_ref, s32[512,16,128]{2,1,0:T(8,128)} %rows_ref.1, bf16[1024,256]{1,0:T(8,128)(2,1)} %pad_maximum_fusion.win_ref), custom_call_target="tpu_custom_call" | custom-call | tf_op jit(solution)/shard_map/pallas_call | solution.py:48
  21.7 1.1 %fusion.4 = bf16[512,128]{1,0:T(8,128)(2,1)S(1)} fusion(f32[512,256]{1,0:T(8,128)} %shard_map.86, f32[512]{0:T(512)S(1)} %convert_divide_fusion), kind=kLoop, calls=%fused_computation.12 | loop fusion | flops 131072 | bytes 395264 | tf_op jit(solution)/shard_map/convert_element_type | solution.py:84
  22.8 1.0 %slice.80 = bf16[512,128]{1,0:T(8,128)(2,1)S(1)} slice(f32[512,256]{1,0:T(8,128)} %shard_map.86), slice={[0:512], [128:256]} | slice | bytes 262144 | tf_op jit(solution)/shard_map/slice | solution.py:85
  23.8 1.0 %copy.24 = bf16[4,128,512]{1,2,0:T(8,128)(2,1)} copy(bf16[4,128,512]{2,1,0:T(8,128)(2,1)S(1)} %bitcast.64) | data formatting | bytes 1048576 | tf_op jit(solution)/shard_map/all_to_all | solution.py:23
  24.8 14.5 %all-to-all-start = ((bf16[4,128,512]{1,2,0:T(8,128)(2,1)}), bf16[4,128,512]{1,2,0:T(8,128)(2,1)S(1)}, u32[]{:S(2)}, u32[]{:S(2)}) async-start(bf16[4,128,512]{1,2,0:T(8,128)(2,1)} %copy.24), calls=%async_computation | async-start | bytes 1048576 | tf_op jit(solution)/shard_map/all_to_all | solution.py:23
  39.3 0.2 copy.36
  39.6 0.2 copy.35
  39.8 23.1 %all-to-all-done = bf16[4,128,512]{1,2,0:T(8,128)(2,1)S(1)} async-done(((bf16[4,128,512]{1,2,0:T(8,128)(2,1)}), bf16[4,128,512]{1,2,0:T(8,128)(2,1)S(1)}, u32[]{:S(2)}, u32[]{:S(2)}) %all-to-all-start) | async-done | bytes 524320 | tf_op jit(solution)/shard_map/all_to_all | solution.py:23
  62.8 0.2 convolution_bitcast_fusion.2
  63.1 0.3 fusion.3
  63.5 0.3 convolution_bitcast_fusion
  63.7 0.3 fusion.2
  64.2 19.9 %all_to_all.18 = bf16[4,128,256]{1,2,0:T(8,128)(2,1)S(1)} all-to-all(bf16[4,128,256]{1,2,0:T(8,128)(2,1)S(1)} %bitcast.69), channel_id=1, replica_groups=mesh['row'=192,'col'=4] {'col'}, dimensions={0} | all-to-all | bytes 524288 | tf_op jit(solution)/shard_map/all_to_all | solution.py:23
  84.3 0.4 fusion.6
  84.7 0.7 copy_bitcast_fusion
  (17 shorter events, 0.7 us)
Async XLA Ops:
  0.6 23.1 %copy-start.3 = (bf16[512,128]{1,0:T(8,128)(2,1)S(1)}, bf16[512,128]{1,0:T(8,128)(2,1)}, u32[]{:S(2)}) copy-start(bf16[512,128]{1,0:T(8,128)(2,1)} %param.8) | copy-start | bytes 393220
  0.6 23.1 %copy-start.2 = (bf16[512,128]{1,0:T(8,128)(2,1)S(1)}, bf16[512,128]{1,0:T(8,128)(2,1)}, u32[]{:S(2)}) copy-start(bf16[512,128]{1,0:T(8,128)(2,1)} %param.7) | copy-start | bytes 393220
  3.3 7.1 %collective-permute-start = (bf16[256,256]{1,0:T(8,128)(2,1)S(1)}, bf16[256,256]{1,0:T(8,128)(2,1)S(1)}, u32[]{:S(2)}, u32[]{:S(2)}) collective-permute-start(bf16[256,256]{1,0:T(8,128)(2,1)S(1)} %get-tuple-element.4), channel_id=1, source_target_pairs={{0,4},{4,8},{8,12},{12,16},{16,20},{20,24},{24,28},{28,32},{32,36}... | collective-permute-start | bytes 393224 | tf_op jit(solution)/shard_map/ppermute | solution.py:17
  5.3 6.1 %collective-permute-start.1 = (bf16[256,256]{1,0:T(8,128)(2,1)S(1)}, bf16[256,256]{1,0:T(8,128)(2,1)S(1)}, u32[]{:S(2)}, u32[]{:S(2)}) collective-permute-start(bf16[256,256]{1,0:T(8,128)(2,1)S(1)} %get-tuple-element.5), channel_id=1, source_target_pairs={{4,0},{8,4},{12,8},{16,12},{20,16},{24,20},{28,24},{32,28},{36,32}... | collective-permute-start | bytes 393224 | tf_op jit(solution)/shard_map/ppermute | solution.py:17
  13.2 26.2 %copy-start = (bf16[512,512]{1,0:T(8,128)(2,1)S(1)}, bf16[512,512]{1,0:T(8,128)(2,1)}, u32[]{:S(2)}) copy-start(bf16[512,512]{1,0:T(8,128)(2,1)} %param.10) | copy-start | bytes 1572868
  13.2 26.4 %copy-start.1 = (bf16[512,512]{1,0:T(8,128)(2,1)S(1)}, bf16[512,512]{1,0:T(8,128)(2,1)}, u32[]{:S(2)}) copy-start(bf16[512,512]{1,0:T(8,128)(2,1)} %param.9) | copy-start | bytes 1572868
  24.8 38.0 %all-to-all-start = ((bf16[4,128,512]{1,2,0:T(8,128)(2,1)}), bf16[4,128,512]{1,2,0:T(8,128)(2,1)S(1)}, u32[]{:S(2)}, u32[]{:S(2)}) async-start(bf16[4,128,512]{1,2,0:T(8,128)(2,1)} %copy.24), calls=%async_computation | async-start | bytes 1048576 | tf_op jit(solution)/shard_map/all_to_all | solution.py:23

commit v6 on v4

--- a/solution.py
+++ b/solution.py
@@ -2,6 +2,7 @@
 import jax.numpy as jnp
 from jax import lax
 from jax.sharding import PartitionSpec as P
+from jax.experimental.layout import Layout, with_layout_constraint
 
 USE_ALL_TO_ALL = True
 
@@ -41,6 +42,7 @@
     from_prev = shifted(pair[rows_here - reach:], "row", 1)
     from_next = shifted(pair[:reach], "row", -1)
     window = jnp.concatenate([from_prev, pair, from_next], axis=0)
+    window = with_layout_constraint(window, Layout(major_to_minor=(0, 1)))
     window_blocks = window.shape[0] // block
     first_block = lax.axis_index("row") * (rows_here // block) - reach // block
     blocks_here = rows_here // block

time: 73.3 us -> 75.1 us (1.025)
  the two profiles are of different devices: /device:TPU:111 before, /device:TPU:31 now
where the time goes in v6:
time: 75.1 us; the launch traced here: 74.7 us
  waiting for transfers between devices  25.2 us (34%)
  starting transfers between devices  21 us (28%)
  blocking collectives  17.1 us (23%)
  other arithmetic  5.34 us (7%)
  local copies, waits for them, and re-layouts  3.41 us (5%)
  matrix products  1.87 us (2%)
  between operations  0.82 us (1%)
    all_to_all x1, waiting for transfers between devices, swap_chunks(): return lax.all_to_all(block, axis, 0, 0, tiled=True)  20.6 us
    all_to_all x1, blocking collectives, swap_chunks(): return lax.all_to_all(block, axis, 0, 0, tiled=True)  17.1 us
    all_to_all x1, starting transfers between devices, swap_chunks(): return lax.all_to_all(block, axis, 0, 0, tiled=True)  14.2 us
    ppermute x2, starting transfers between devices, shifted(): return lax.ppermute(block, axis, route)  6.81 us
    ppermute x2, waiting for transfers between devices, shifted(): return lax.ppermute(block, axis, route)  4.6 us
    convert_element_type x1, other arithmetic, per_device(): tile_rows.astype(jnp.bfloat16).reshape(blocks_here, block, -1, block)  2.47 us
  transfers between devices with their start and end apart: 3, of which 2 were waited for; matrix products, arithmetic and copies ran while one was open for 5% of the time, Pallas kernels for 0%

profile of v6, /device:TPU:31, one launch (start us, length us, event | category | flops | bytes accessed | tf_op | source)
XLA Modules:
  0.0 74.7 jit_solution(10824678707587833471)
XLA Ops:
  0.6 0.7 convert_divide_fusion
  1.3 1.0 %multiply_convert_fusion = bf16[512,128]{1,0:T(8,128)(2,1)S(1)} fusion(bf16[512,128]{1,0:T(8,128)(2,1)} %param.8, f32[512]{0:T(512)S(1)} %convert_divide_fusion), kind=kLoop, calls=%fused_computation.26 | loop fusion | flops 196608 | bytes 264192 | tf_op jit(solution)/shard_map/convert_element_type | solution.py:38
  2.4 0.9 %fusion.15 = (bf16[256,256]{1,0:T(8,128)(2,1)S(1)}, bf16[256,256]{1,0:T(8,128)(2,1)S(1)}) fusion(bf16[512,128]{1,0:T(8,128)(2,1)} %param.7, bf16[512,128]{1,0:T(8,128)(2,1)S(1)} %multiply_convert_fusion), kind=kLoop, calls=%fused_computation.27 | loop fusion | flops 524288 | bytes 524288 | tf_op jit(solution)/shard_map/concatenate | solution.py:41
  3.3 4.9 %collective-permute-start = (bf16[256,256]{1,0:T(8,128)(2,1)S(1)}, bf16[256,256]{1,0:T(8,128)(2,1)S(1)}, u32[]{:S(2)}, u32[]{:S(2)}) collective-permute-start(bf16[256,256]{1,0:T(8,128)(2,1)S(1)} %get-tuple-element.4), channel_id=1, source_target_pairs={{0,4},{4,8},{8,12},{12,16},{16,20},{20,24},{24,28},{28,32},{32,36}... | collective-permute-start | bytes 393224 | tf_op jit(solution)/shard_map/ppermute | solution.py:13
  8.2 1.9 %collective-permute-start.1 = (bf16[256,256]{1,0:T(8,128)(2,1)S(1)}, bf16[256,256]{1,0:T(8,128)(2,1)S(1)}, u32[]{:S(2)}, u32[]{:S(2)}) collective-permute-start(bf16[256,256]{1,0:T(8,128)(2,1)S(1)} %get-tuple-element.5), channel_id=1, source_target_pairs={{4,0},{8,4},{12,8},{16,12},{20,16},{24,20},{28,24},{32,28},{36,32}... | collective-permute-start | bytes 393224 | tf_op jit(solution)/shard_map/ppermute | solution.py:13
  10.1 2.5 %convert_element_type.29 = bf16[512,16,128]{2,1,0:T(8,128)(2,1)S(1)} convert(s32[512,16,128]{2,1,0:T(8,128)} %param.11) | non-fusion elementwise | flops 1048576 | bytes 6291456 | tf_op jit(solution)/shard_map/convert_element_type | solution.py:53
  12.7 0.4 convolution_convert_fusion
  13.2 4.6 %collective-permute-done.1 = bf16[256,256]{1,0:T(8,128)(2,1)S(1)} collective-permute-done((bf16[256,256]{1,0:T(8,128)(2,1)S(1)}, bf16[256,256]{1,0:T(8,128)(2,1)S(1)}, u32[]{:S(2)}, u32[]{:S(2)}) %collective-permute-start.1) | collective-permute-done | bytes 131104 | tf_op jit(solution)/shard_map/ppermute | solution.py:13
  17.8 0.4 fusion.4
  18.2 0.1 fusion.14
  18.4 0.3 copy-done.2
  18.8 1.0 %copy.30 = bf16[4,128,512]{1,2,0:T(8,128)(2,1)} copy(bf16[4,128,512]{2,1,0:T(8,128)(2,1)S(1)} %bitcast.78) | data formatting | bytes 1048576 | tf_op jit(solution)/shard_map/all_to_all | solution.py:19
  19.8 14.2 %all-to-all-start = ((bf16[4,128,512]{1,2,0:T(8,128)(2,1)}), bf16[4,128,512]{1,2,0:T(8,128)(2,1)S(1)}, u32[]{:S(2)}, u32[]{:S(2)}) async-start(bf16[4,128,512]{1,2,0:T(8,128)(2,1)} %copy.30), calls=%async_computation | async-start | bytes 1048576 | tf_op jit(solution)/shard_map/all_to_all | solution.py:19
  34.0 0.2 copy.44
  34.2 0.2 copy.43
  34.4 20.6 %all-to-all-done = bf16[4,128,512]{1,2,0:T(8,128)(2,1)S(1)} async-done(((bf16[4,128,512]{1,2,0:T(8,128)(2,1)}), bf16[4,128,512]{1,2,0:T(8,128)(2,1)S(1)}, u32[]{:S(2)}, u32[]{:S(2)}) %all-to-all-start) | async-done | bytes 524320 | tf_op jit(solution)/shard_map/all_to_all | solution.py:19
  55.0 0.2 convolution_bitcast_fusion.2
  55.3 0.3 fusion.3
  55.7 0.3 convolution_bitcast_fusion
  55.9 0.3 fusion.2
  56.3 17.1 %all_to_all.18 = bf16[4,128,256]{1,2,0:T(8,128)(2,1)S(1)} all-to-all(bf16[4,128,256]{1,2,0:T(8,128)(2,1)S(1)} %bitcast.83), channel_id=1, replica_groups=mesh['row'=192,'col'=4] {'col'}, dimensions={0} | all-to-all | bytes 524288 | tf_op jit(solution)/shard_map/all_to_all | solution.py:19
  73.4 0.1 copy.39
  73.6 0.4 fusion.20
  74.0 0.7 copy_bitcast_fusion
  (19 shorter events, 0.6 us)
Async XLA Ops:
  3.3 9.9 %collective-permute-start = (bf16[256,256]{1,0:T(8,128)(2,1)S(1)}, bf16[256,256]{1,0:T(8,128)(2,1)S(1)}, u32[]{:S(2)}, u32[]{:S(2)}) collective-permute-start(bf16[256,256]{1,0:T(8,128)(2,1)S(1)} %get-tuple-element.4), channel_id=1, source_target_pairs={{0,4},{4,8},{8,12},{12,16},{16,20},{20,24},{24,28},{28,32},{32,36}... | collective-permute-start | bytes 393224 | tf_op jit(solution)/shard_map/ppermute | solution.py:13
  8.2 9.6 %collective-permute-start.1 = (bf16[256,256]{1,0:T(8,128)(2,1)S(1)}, bf16[256,256]{1,0:T(8,128)(2,1)S(1)}, u32[]{:S(2)}, u32[]{:S(2)}) collective-permute-start(bf16[256,256]{1,0:T(8,128)(2,1)S(1)} %get-tuple-element.5), channel_id=1, source_target_pairs={{4,0},{8,4},{12,8},{16,12},{20,16},{24,20},{28,24},{32,28},{36,32}... | collective-permute-start | bytes 393224 | tf_op jit(solution)/shard_map/ppermute | solution.py:13
  10.1 2.5 %copy-start.4 = (s32[512,16]{0,1:T(8,128)S(1)}, s32[512,16]{0,1:T(8,128)}, u32[]{:S(2)}) copy-start(s32[512,16]{0,1:T(8,128)} %param.12) | copy-start | bytes 98308
  12.6 5.2 %copy-start.3 = (bf16[512,128]{1,0:T(8,128)(2,1)S(1)}, bf16[512,128]{1,0:T(8,128)(2,1)}, u32[]{:S(2)}) copy-start(bf16[512,128]{1,0:T(8,128)(2,1)} %param.7) | copy-start | bytes 393220
  17.8 0.9 %copy-start.2 = (bf16[512,128]{1,0:T(8,128)(2,1)S(1)}, bf16[512,128]{1,0:T(8,128)(2,1)}, u32[]{:S(2)}) copy-start(bf16[512,128]{1,0:T(8,128)(2,1)} %param.8) | copy-start | bytes 393220
  18.2 15.8 %copy-start = (bf16[512,512]{1,0:T(8,128)(2,1)S(1)}, bf16[512,512]{1,0:T(8,128)(2,1)}, u32[]{:S(2)}) copy-start(bf16[512,512]{1,0:T(8,128)(2,1)} %param.10) | copy-start | bytes 1572868
  18.7 15.5 %copy-start.1 = (bf16[512,512]{1,0:T(8,128)(2,1)S(1)}, bf16[512,512]{1,0:T(8,128)(2,1)}, u32[]{:S(2)}) copy-start(bf16[512,512]{1,0:T(8,128)(2,1)} %param.9) | copy-start | bytes 1572868
  19.8 35.3 %all-to-all-start = ((bf16[4,128,512]{1,2,0:T(8,128)(2,1)}), bf16[4,128,512]{1,2,0:T(8,128)(2,1)S(1)}, u32[]{:S(2)}, u32[]{:S(2)}) async-start(bf16[4,128,512]{1,2,0:T(8,128)(2,1)} %copy.30), calls=%async_computation | async-start | bytes 1048576 | tf_op jit(solution)/shard_map/all_to_all | solution.py:19

commit v7 on v4

--- a/solution.py
+++ b/solution.py
@@ -36,6 +36,8 @@
     inverse = 1.0 / degree.astype(jnp.float32)
     scaled = (out_grad.astype(jnp.float32) * inverse[:, None]).astype(jnp.bfloat16)
 
+    own_in = swap_chunks(jnp.concatenate([features, out_grad], axis=1), "col")
+
     reach = 2 * block
     pair = jnp.concatenate([features, scaled], axis=1)
     from_prev = shifted(pair[rows_here - reach:], "row", 1)
@@ -54,11 +56,9 @@
     sums = jnp.dot(slab, window, preferred_element_type=jnp.float32)
     aggregated = (sums[:, :part] * inverse[:, None]).astype(jnp.bfloat16)
     back_agg = sums[:, part:].astype(jnp.bfloat16)
-    ins = swap_chunks(
-        jnp.concatenate([features, out_grad, aggregated, back_agg], axis=1), "col"
-    ).reshape(n_col, chunk, 4, part)
-    own_in = ins[:, :, :2]
-    agg_in = ins[:, :, 2:]
+    agg_in = swap_chunks(jnp.concatenate([aggregated, back_agg], axis=1), "col")
+    own_in = own_in.reshape(n_col, chunk, 2, part)
+    agg_in = agg_in.reshape(n_col, chunk, 2, part)
     ws = self_weight.reshape(n_col, part, width)
     wn = neigh_weight.reshape(n_col, part, width)
     ws_t = self_weight.T.reshape(n_col, part, width)
@@ -89,6 +89,7 @@
         P("row", None),
         P("row"),
     )
+
     return jax.shard_map(
         per_device,
         mesh=mesh,

time: 73.3 us -> 80.7 us (1.10)
  the two profiles are of different devices: /device:TPU:111 before, /device:TPU:42 now
where the time goes in v7:
time: 80.7 us; the launch traced here: 80.2 us
  waiting for transfers between devices  27.8 us (34%)
  starting transfers between devices  22.2 us (28%)
  blocking collectives  17.4 us (22%)
  other arithmetic  5.71 us (7%)
  local copies, waits for them, and re-layouts  4.31 us (5%)
  matrix products  1.92 us (2%)
  between operations  0.85 us (1%)
    all_to_all x2, waiting for transfers between devices, swap_chunks(): return lax.all_to_all(block, axis, 0, 0, tiled=True)  27.8 us
    all_to_all x2, starting transfers between devices, swap_chunks(): return lax.all_to_all(block, axis, 0, 0, tiled=True)  17.9 us
    all_to_all x1, blocking collectives, swap_chunks(): return lax.all_to_all(block, axis, 0, 0, tiled=True)  17.4 us
    ppermute x2, starting transfers between devices, shifted(): return lax.ppermute(block, axis, route)  4.33 us
    unnamed x10, local copies, waits for them, and re-layouts  2.87 us
    convert_element_type x1, other arithmetic, per_device(): tile_rows.astype(jnp.bfloat16).reshape(blocks_here, block, -1, block)  2.47 us
    concatenate x1, other arithmetic, per_device(): own_in = swap_chunks(jnp.concatenate([features, out_grad], axis=1), 'col')  1.69 us
  transfers between devices with their start and end apart: 4, of which 2 were waited for; matrix products, arithmetic and copies ran while one was open for 8% of the time, Pallas kernels for 0%

profile of v7, /device:TPU:42, one launch (start us, length us, event | category | flops | bytes accessed | tf_op | source)
XLA Modules:
  0.0 80.2 jit_solution(8851916042616491469)
XLA Ops:
  0.6 1.0 %copy.31 = bf16[512,128]{0,1:T(8,128)(2,1)S(1)} copy(bf16[512,128]{1,0:T(8,128)(2,1)} %param.7) | data formatting | bytes 262144 | tf_op args[0]
  1.6 1.0 %copy.30 = bf16[512,128]{0,1:T(8,128)(2,1)S(1)} copy(bf16[512,128]{1,0:T(8,128)(2,1)} %param.8) | data formatting | bytes 262144 | tf_op args[1]
  2.7 0.7 convert_divide_fusion
  3.4 1.9 %collective-permute-start.1 = (bf16[256,256]{0,1:T(8,128)(2,1)S(1)}, bf16[256,256]{0,1:T(8,128)(2,1)S(1)}, u32[]{:S(2)}, u32[]{:S(2)}) collective-permute-start(bf16[256,256]{0,1:T(8,128)(2,1)S(1)} %get-tuple-element.5), channel_id=1, source_target_pairs={{4,0},{8,4},{12,8},{16,12},{20,16},{24,20},{28,24},{32,28},{36,32}... | collective-permute-start | bytes 393224 | tf_op jit(solution)/shard_map/ppermute | solution.py:12
  5.3 2.4 %collective-permute-start = (bf16[256,256]{0,1:T(8,128)(2,1)S(1)}, bf16[256,256]{0,1:T(8,128)(2,1)S(1)}, u32[]{:S(2)}, u32[]{:S(2)}) collective-permute-start(bf16[256,256]{0,1:T(8,128)(2,1)S(1)} %get-tuple-element.4), channel_id=1, source_target_pairs={{0,4},{4,8},{8,12},{12,16},{16,20},{20,24},{24,28},{28,32},{32,36}... | collective-permute-start | bytes 393224 | tf_op jit(solution)/shard_map/ppermute | solution.py:12
  7.8 1.7 %pad_maximum_fusion = bf16[512,256]{1,0:T(8,128)(2,1)} fusion(bf16[512,128]{1,0:T(8,128)(2,1)} %param.8, bf16[512,128]{1,0:T(8,128)(2,1)} %param.7), kind=kLoop, calls=%fused_computation.23 | loop fusion | flops 524288 | bytes 524288 | tf_op jit(solution)/shard_map/concatenate | solution.py:39
  9.4 14.5 %all-to-all-start = ((bf16[4,128,256]{2,1,0:T(8,128)(2,1)}), bf16[4,128,256]{2,1,0:T(8,128)(2,1)S(1)}, u32[]{:S(2)}, u32[]{:S(2)}) async-start(bf16[4,128,256]{2,1,0:T(8,128)(2,1)} %bitcast), calls=%async_computation | async-start | bytes 524288 | tf_op jit(solution)/shard_map/all_to_all | solution.py:18
  23.9 2.5 %convert_element_type.29 = bf16[512,16,128]{2,1,0:T(8,128)(2,1)S(1)} convert(s32[512,16,128]{2,1,0:T(8,128)} %param.11) | non-fusion elementwise | flops 1048576 | bytes 6291456 | tf_op jit(solution)/shard_map/convert_element_type | solution.py:53
  26.6 0.4 convolution_convert_fusion
  27.0 0.5 fusion.4
  27.6 0.8 copy_bitcast_fusion
  28.3 11.9 %all-to-all-done = bf16[4,128,256]{2,1,0:T(8,128)(2,1)S(1)} async-done(((bf16[4,128,256]{2,1,0:T(8,128)(2,1)}), bf16[4,128,256]{2,1,0:T(8,128)(2,1)S(1)}, u32[]{:S(2)}, u32[]{:S(2)}) %all-to-all-start) | async-done | bytes 262176 | tf_op jit(solution)/shard_map/all_to_all | solution.py:18
  40.3 3.4 %all-to-all-start.1 = ((bf16[4,128,256]{1,2,0:T(8,128)(2,1)}), bf16[4,128,256]{1,2,0:T(8,128)(2,1)S(1)}, u32[]{:S(2)}, u32[]{:S(2)}) async-start(bf16[4,128,256]{1,2,0:T(8,128)(2,1)} %copy_bitcast_fusion), calls=%async_computation.1 | async-start | bytes 524288 | tf_op jit(solution)/shard_map/all_to_all | solution.py:18
  43.7 0.2 copy.44
  43.9 0.2 copy.43
  44.1 0.2 copy.27
  44.3 15.9 %all-to-all-done.1 = bf16[4,128,256]{1,2,0:T(8,128)(2,1)S(1)} async-done(((bf16[4,128,256]{1,2,0:T(8,128)(2,1)}), bf16[4,128,256]{1,2,0:T(8,128)(2,1)S(1)}, u32[]{:S(2)}, u32[]{:S(2)}) %all-to-all-start.1) | async-done | bytes 262176 | tf_op jit(solution)/shard_map/all_to_all | solution.py:18
  60.2 0.2 convolution_bitcast_fusion
  60.4 0.3 fusion.2
  60.8 0.3 convolution_bitcast_fusion.2
  61.1 0.3 fusion.3
  61.5 17.4 %all_to_all.27 = bf16[4,128,256]{1,2,0:T(8,128)(2,1)S(1)} all-to-all(bf16[4,128,256]{1,2,0:T(8,128)(2,1)S(1)} %bitcast.86), channel_id=1, replica_groups=mesh['row'=192,'col'=4] {'col'}, dimensions={0} | all-to-all | bytes 524288 | tf_op jit(solution)/shard_map/all_to_all | solution.py:18
  79.1 0.4 fusion.20
  79.5 0.7 copy_bitcast_fusion.1
  (20 shorter events, 0.7 us)
Async XLA Ops:
  3.4 23.6 %collective-permute-start.1 = (bf16[256,256]{0,1:T(8,128)(2,1)S(1)}, bf16[256,256]{0,1:T(8,128)(2,1)S(1)}, u32[]{:S(2)}, u32[]{:S(2)}) collective-permute-start(bf16[256,256]{0,1:T(8,128)(2,1)S(1)} %get-tuple-element.5), channel_id=1, source_target_pairs={{4,0},{8,4},{12,8},{16,12},{20,16},{24,20},{28,24},{32,28},{36,32}... | collective-permute-start | bytes 393224 | tf_op jit(solution)/shard_map/ppermute | solution.py:12
  5.3 21.7 %collective-permute-start = (bf16[256,256]{0,1:T(8,128)(2,1)S(1)}, bf16[256,256]{0,1:T(8,128)(2,1)S(1)}, u32[]{:S(2)}, u32[]{:S(2)}) collective-permute-start(bf16[256,256]{0,1:T(8,128)(2,1)S(1)} %get-tuple-element.4), channel_id=1, source_target_pairs={{0,4},{4,8},{8,12},{12,16},{16,20},{20,24},{24,28},{28,32},{32,36}... | collective-permute-start | bytes 393224 | tf_op jit(solution)/shard_map/ppermute | solution.py:12
  9.4 30.8 %all-to-all-start = ((bf16[4,128,256]{2,1,0:T(8,128)(2,1)}), bf16[4,128,256]{2,1,0:T(8,128)(2,1)S(1)}, u32[]{:S(2)}, u32[]{:S(2)}) async-start(bf16[4,128,256]{2,1,0:T(8,128)(2,1)} %bitcast), calls=%async_computation | async-start | bytes 524288 | tf_op jit(solution)/shard_map/all_to_all | solution.py:18
  23.9 2.5 %copy-start.2 = (s32[512,16]{0,1:T(8,128)S(1)}, s32[512,16]{0,1:T(8,128)}, u32[]{:S(2)}) copy-start(s32[512,16]{0,1:T(8,128)} %param.12) | copy-start | bytes 98308
  27.0 16.7 %copy-start = (bf16[512,512]{1,0:T(8,128)(2,1)S(1)}, bf16[512,512]{1,0:T(8,128)(2,1)}, u32[]{:S(2)}) copy-start(bf16[512,512]{1,0:T(8,128)(2,1)} %param.10) | copy-start | bytes 1572868
  27.5 16.4 %copy-start.1 = (bf16[512,512]{1,0:T(8,128)(2,1)S(1)}, bf16[512,512]{1,0:T(8,128)(2,1)}, u32[]{:S(2)}) copy-start(bf16[512,512]{1,0:T(8,128)(2,1)} %param.9) | copy-start | bytes 1572868
  40.3 19.9 %all-to-all-start.1 = ((bf16[4,128,256]{1,2,0:T(8,128)(2,1)}), bf16[4,128,256]{1,2,0:T(8,128)(2,1)S(1)}, u32[]{:S(2)}, u32[]{:S(2)}) async-start(bf16[4,128,256]{1,2,0:T(8,128)(2,1)} %copy_bitcast_fusion), calls=%async_computation.1 | async-start | bytes 524288 | tf_op jit(solution)/shard_map/all_to_all | solution.py:18

commit v8 on v4

--- a/solution.py
+++ b/solution.py
@@ -74,9 +74,9 @@
     both = jnp.stack(
         [output.astype(jnp.bfloat16), feature_grad.astype(jnp.bfloat16)], axis=0
     )
-    both = both.reshape(2, chunk, n_col, part).transpose(2, 1, 0, 3).reshape(n_col * chunk, 2 * part)
-    back = swap_chunks(both, "col").reshape(rows_here, 2, part)
-    return (back[:, 0], back[:, 1])
+    both = both.reshape(2, chunk, n_col, part).transpose(2, 0, 1, 3)
+    back = lax.all_to_all(both, "col", 0, 0, tiled=True)
+    return (back[:, 0].reshape(rows_here, part), back[:, 1].reshape(rows_here, part))
 
 
 def solution(mesh):

time: 73.3 us -> 72.7 us (level)
  the two profiles are of different devices: /device:TPU:111 before, /device:TPU:71 now
where the time goes in v8:
time: 72.7 us; the launch traced here: 72.4 us
  waiting for transfers between devices  22.8 us (31%)
  starting transfers between devices  21 us (29%)
  blocking collectives  18.3 us (25%)
  other arithmetic  4.15 us (6%)
  local copies, waits for them, and re-layouts  3.42 us (5%)
  matrix products  1.9 us (3%)
  between operations  0.84 us (1%)
    all_to_all x1, waiting for transfers between devices, swap_chunks(): return lax.all_to_all(block, axis, 0, 0, tiled=True)  22.8 us
    all_to_all x1, blocking collectives, per_device(): back = lax.all_to_all(both, 'col', 0, 0, tiled=True)  18.3 us
    all_to_all x1, starting transfers between devices, swap_chunks(): return lax.all_to_all(block, axis, 0, 0, tiled=True)  13.3 us
    ppermute x2, starting transfers between devices, shifted(): return lax.ppermute(block, axis, route)  7.67 us
    convert_element_type x1, other arithmetic, per_device(): tile_rows.astype(jnp.bfloat16).reshape(blocks_here, block, -1, block)  2.47 us
    unnamed x9, local copies, waits for them, and re-layouts  2.13 us
  transfers between devices with their start and end apart: 3, of which 1 were waited for; matrix products, arithmetic and copies ran while one was open for 5% of the time, Pallas kernels for 0%

profile of v8, /device:TPU:71, one launch (start us, length us, event | category | flops | bytes accessed | tf_op | source)
XLA Modules:
  0.0 72.4 jit_solution(16190923388019315161)
XLA Ops:
  0.6 1.0 %copy.35 = bf16[512,128]{0,1:T(8,128)(2,1)S(1)} copy(bf16[512,128]{1,0:T(8,128)(2,1)} %param.7) | data formatting | bytes 262144 | tf_op args[0]
  1.6 1.0 %copy.36 = bf16[512,128]{0,1:T(8,128)(2,1)S(1)} copy(bf16[512,128]{1,0:T(8,128)(2,1)} %param.8) | data formatting | bytes 262144 | tf_op args[1]
  2.7 0.7 convert_divide_fusion
  3.4 2.6 %collective-permute-start.1 = (bf16[256,256]{0,1:T(8,128)(2,1)S(1)}, bf16[256,256]{0,1:T(8,128)(2,1)S(1)}, u32[]{:S(2)}, u32[]{:S(2)}) collective-permute-start(bf16[256,256]{0,1:T(8,128)(2,1)S(1)} %get-tuple-element.5), channel_id=1, source_target_pairs={{4,0},{8,4},{12,8},{16,12},{20,16},{24,20},{28,24},{32,28},{36,32}... | collective-permute-start | bytes 393224 | tf_op jit(solution)/shard_map/ppermute | solution.py:12
  6.0 5.1 %collective-permute-start = (bf16[256,256]{0,1:T(8,128)(2,1)S(1)}, bf16[256,256]{0,1:T(8,128)(2,1)S(1)}, u32[]{:S(2)}, u32[]{:S(2)}) collective-permute-start(bf16[256,256]{0,1:T(8,128)(2,1)S(1)} %get-tuple-element.4), channel_id=1, source_target_pairs={{0,4},{4,8},{8,12},{12,16},{16,20},{20,24},{24,28},{28,32},{32,36}... | collective-permute-start | bytes 393224 | tf_op jit(solution)/shard_map/ppermute | solution.py:12
  11.1 0.0 copy-start.2
  11.1 2.5 %convert_element_type.29 = bf16[512,16,128]{2,1,0:T(8,128)(2,1)S(1)} convert(s32[512,16,128]{2,1,0:T(8,128)} %param.11) | non-fusion elementwise | flops 1048576 | bytes 6291456 | tf_op jit(solution)/shard_map/convert_element_type | solution.py:51
  13.6 0.1 copy.49
  13.7 0.4 convolution_convert_fusion
  14.2 0.0 collective-permute-done.1
  14.2 0.5 fusion.4
  14.7 0.0 copy-start
  14.7 0.0 copy-start.1
  14.7 0.9 %copy_bitcast_fusion = bf16[4,128,512]{1,2,0:T(8,128)(2,1)} fusion(bf16[512,128]{0,1:T(8,128)(2,1)S(1)} %slice.80, bf16[512,128]{0,1:T(8,128)(2,1)S(1)} %fusion.14, bf16[512,128]{0,1:T(8,128)(2,1)S(1)} %copy.36, bf16[512,128]{0,1:T(8,128)(2,1)S(1)} %copy.35), kind=kLoop, calls=%fused_computation.12 | loop fusion | flops 2097152 | bytes 1048576 | tf_op jit(solution)/shard_map/all_to_all | solution.py:18
  15.6 13.3 %all-to-all-start = ((bf16[4,128,512]{1,2,0:T(8,128)(2,1)}), bf16[4,128,512]{1,2,0:T(8,128)(2,1)S(1)}, u32[]{:S(2)}, u32[]{:S(2)}) async-start(bf16[4,128,512]{1,2,0:T(8,128)(2,1)} %copy_bitcast_fusion), calls=%async_computation | async-start | bytes 1048576 | tf_op jit(solution)/shard_map/all_to_all | solution.py:18
  29.0 0.2 copy.48
  29.2 0.2 copy.47
  29.4 22.8 %all-to-all-done = bf16[4,128,512]{1,2,0:T(8,128)(2,1)S(1)} async-done(((bf16[4,128,512]{1,2,0:T(8,128)(2,1)}), bf16[4,128,512]{1,2,0:T(8,128)(2,1)S(1)}, u32[]{:S(2)}, u32[]{:S(2)}) %all-to-all-start) | async-done | bytes 524320 | tf_op jit(solution)/shard_map/all_to_all | solution.py:18
  52.2 0.2 convolution_bitcast_fusion
  52.4 0.3 fusion.2
  52.8 0.2 convolution_bitcast_fusion.2
  53.0 0.3 fusion.3
  53.4 18.3 %all_to_all.14 = bf16[4,2,128,128]{3,2,1,0:T(8,128)(2,1)S(1)} all-to-all(bf16[4,2,128,128]{3,2,1,0:T(8,128)(2,1)S(1)} %maximum_bitcast_fusion.1), channel_id=1, replica_groups=mesh['row'=192,'col'=4] {'col'}, dimensions={0} | all-to-all | bytes 524288 | tf_op jit(solution)/shard_map/all_to_all | solution.py:78
  71.7 0.7 fusion.20
  (15 shorter events, 0.3 us)
Async XLA Ops:
  3.4 10.7 %collective-permute-start.1 = (bf16[256,256]{0,1:T(8,128)(2,1)S(1)}, bf16[256,256]{0,1:T(8,128)(2,1)S(1)}, u32[]{:S(2)}, u32[]{:S(2)}) collective-permute-start(bf16[256,256]{0,1:T(8,128)(2,1)S(1)} %get-tuple-element.5), channel_id=1, source_target_pairs={{4,0},{8,4},{12,8},{16,12},{20,16},{24,20},{28,24},{32,28},{36,32}... | collective-permute-start | bytes 393224 | tf_op jit(solution)/shard_map/ppermute | solution.py:12
  6.0 8.2 %collective-permute-start = (bf16[256,256]{0,1:T(8,128)(2,1)S(1)}, bf16[256,256]{0,1:T(8,128)(2,1)S(1)}, u32[]{:S(2)}, u32[]{:S(2)}) collective-permute-start(bf16[256,256]{0,1:T(8,128)(2,1)S(1)} %get-tuple-element.4), channel_id=1, source_target_pairs={{0,4},{4,8},{8,12},{12,16},{16,20},{20,24},{24,28},{28,32},{32,36}... | collective-permute-start | bytes 393224 | tf_op jit(solution)/shard_map/ppermute | solution.py:12
  11.1 2.5 %copy-start.2 = (s32[512,16]{0,1:T(8,128)S(1)}, s32[512,16]{0,1:T(8,128)}, u32[]{:S(2)}) copy-start(s32[512,16]{0,1:T(8,128)} %param.12) | copy-start | bytes 98308
  14.7 14.3 %copy-start = (bf16[512,512]{1,0:T(8,128)(2,1)S(1)}, bf16[512,512]{1,0:T(8,128)(2,1)}, u32[]{:S(2)}) copy-start(bf16[512,512]{1,0:T(8,128)(2,1)} %param.10) | copy-start | bytes 1572868
  14.7 14.5 %copy-start.1 = (bf16[512,512]{1,0:T(8,128)(2,1)S(1)}, bf16[512,512]{1,0:T(8,128)(2,1)}, u32[]{:S(2)}) copy-start(bf16[512,512]{1,0:T(8,128)(2,1)} %param.9) | copy-start | bytes 1572868
  15.6 36.6 %all-to-all-start = ((bf16[4,128,512]{1,2,0:T(8,128)(2,1)}), bf16[4,128,512]{1,2,0:T(8,128)(2,1)S(1)}, u32[]{:S(2)}, u32[]{:S(2)}) async-start(bf16[4,128,512]{1,2,0:T(8,128)(2,1)} %copy_bitcast_fusion), calls=%async_computation | async-start | bytes 1048576 | tf_op jit(solution)/shard_map/all_to_all | solution.py:18

commit v9 on v8

--- a/solution.py
+++ b/solution.py
@@ -54,11 +54,11 @@
     sums = jnp.dot(slab, window, preferred_element_type=jnp.float32)
     aggregated = (sums[:, :part] * inverse[:, None]).astype(jnp.bfloat16)
     back_agg = sums[:, part:].astype(jnp.bfloat16)
-    ins = swap_chunks(
-        jnp.concatenate([features, out_grad, aggregated, back_agg], axis=1), "col"
-    ).reshape(n_col, chunk, 4, part)
-    own_in = ins[:, :, :2]
-    agg_in = ins[:, :, 2:]
+    ins = jnp.stack([features, out_grad, aggregated, back_agg], axis=0)
+    ins = ins.reshape(4, n_col, chunk, part).transpose(1, 0, 2, 3)
+    ins = lax.all_to_all(ins, "col", 0, 0, tiled=True)
+    own_in = ins[:, :2].transpose(0, 2, 1, 3)
+    agg_in = ins[:, 2:].transpose(0, 2, 1, 3)
     ws = self_weight.reshape(n_col, part, width)
     wn = neigh_weight.reshape(n_col, part, width)
     ws_t = self_weight.T.reshape(n_col, part, width)

time: 72.7 us -> 73.3 us (level)
  the two profiles are of different devices: /device:TPU:71 before, /device:TPU:111 now
where the time goes in v9:
time: 73.3 us; the launch traced here: 72.9 us
  waiting for transfers between devices  26.3 us (36%)
  starting transfers between devices  18 us (25%)
  blocking collectives  18 us (25%)
  other arithmetic  6.13 us (8%)
  matrix products  1.79 us (2%)
  local copies, waits for them, and re-layouts  1.76 us (2%)
  between operations  0.84 us (1%)
    all_to_all x1, waiting for transfers between devices, per_device(): ins = lax.all_to_all(ins, 'col', 0, 0, tiled=True)  22.9 us
    all_to_all x1, blocking collectives, per_device(): back = lax.all_to_all(both, 'col', 0, 0, tiled=True)  18 us
    all_to_all x1, starting transfers between devices, per_device(): ins = lax.all_to_all(ins, 'col', 0, 0, tiled=True)  13.3 us
    ppermute x2, starting transfers between devices, shifted(): return lax.ppermute(block, axis, route)  4.7 us
    ppermute x2, waiting for transfers between devices, shifted(): return lax.ppermute(block, axis, route)  3.39 us
    convert_element_type x1, other arithmetic, per_device(): tile_rows.astype(jnp.bfloat16).reshape(blocks_here, block, -1, block)  2.47 us
  transfers between devices with their start and end apart: 3, of which 2 were waited for; matrix products, arithmetic and copies ran while one was open for 5% of the time, Pallas kernels for 0%

profile of v9, /device:TPU:111, one launch (start us, length us, event | category | flops | bytes accessed | tf_op | source)
XLA Modules:
  0.0 72.9 jit_solution(17193856233479945410)
XLA Ops:
  0.6 0.7 convert_divide_fusion
  1.3 1.0 %multiply_convert_fusion = bf16[512,128]{1,0:T(8,128)(2,1)S(1)} fusion(bf16[512,128]{1,0:T(8,128)(2,1)} %param.8, f32[512]{0:T(512)S(1)} %convert_divide_fusion), kind=kLoop, calls=%fused_computation.28 | loop fusion | flops 196608 | bytes 264192 | tf_op jit(solution)/shard_map/convert_element_type | solution.py:37
  2.4 0.9 %fusion.15 = (bf16[256,256]{1,0:T(8,128)(2,1)S(1)}, bf16[256,256]{1,0:T(8,128)(2,1)S(1)}) fusion(bf16[512,128]{1,0:T(8,128)(2,1)} %param.7, bf16[512,128]{1,0:T(8,128)(2,1)S(1)} %multiply_convert_fusion), kind=kLoop, calls=%fused_computation.29 | loop fusion | flops 524288 | bytes 524288 | tf_op jit(solution)/shard_map/concatenate | solution.py:40
  3.3 2.8 %collective-permute-start = (bf16[256,256]{1,0:T(8,128)(2,1)S(1)}, bf16[256,256]{1,0:T(8,128)(2,1)S(1)}, u32[]{:S(2)}, u32[]{:S(2)}) collective-permute-start(bf16[256,256]{1,0:T(8,128)(2,1)S(1)} %get-tuple-element.6), channel_id=1, source_target_pairs={{0,4},{4,8},{8,12},{12,16},{16,20},{20,24},{24,28},{28,32},{32,36}... | collective-permute-start | bytes 393224 | tf_op jit(solution)/shard_map/ppermute | solution.py:12
  6.1 1.9 %collective-permute-start.1 = (bf16[256,256]{1,0:T(8,128)(2,1)S(1)}, bf16[256,256]{1,0:T(8,128)(2,1)S(1)}, u32[]{:S(2)}, u32[]{:S(2)}) collective-permute-start(bf16[256,256]{1,0:T(8,128)(2,1)S(1)} %get-tuple-element.7), channel_id=1, source_target_pairs={{4,0},{8,4},{12,8},{16,12},{20,16},{24,20},{28,24},{32,28},{36,32}... | collective-permute-start | bytes 393224 | tf_op jit(solution)/shard_map/ppermute | solution.py:12
  8.0 2.5 %convert_element_type.29 = bf16[512,16,128]{2,1,0:T(8,128)(2,1)S(1)} convert(s32[512,16,128]{2,1,0:T(8,128)} %param.11) | non-fusion elementwise | flops 1048576 | bytes 6291456 | tf_op jit(solution)/shard_map/convert_element_type | solution.py:51
  10.5 0.1 copy.26
  10.6 0.4 convolution_convert_fusion
  11.1 3.4 %collective-permute-done.1 = bf16[256,256]{1,0:T(8,128)(2,1)S(1)} collective-permute-done((bf16[256,256]{1,0:T(8,128)(2,1)S(1)}, bf16[256,256]{1,0:T(8,128)(2,1)S(1)}, u32[]{:S(2)}, u32[]{:S(2)}) %collective-permute-start.1) | collective-permute-done | bytes 131104 | tf_op jit(solution)/shard_map/ppermute | solution.py:12
  14.5 0.4 fusion.4
  14.9 0.0 copy-start
  14.9 0.1 fusion.14
  15.1 0.3 copy-done.2
  15.4 0.9 %maximum_bitcast_fusion = bf16[4,4,128,128]{3,2,1,0:T(8,128)(2,1)} fusion(bf16[1,4,128,128]{3,2,0,1:T(8,128)(2,1)S(1)} %bitcast.84, bf16[1,4,128,128]{3,2,0,1:T(8,128)(2,1)S(1)} %bitcast.82, bf16[1,4,128,128]{3,2,0,1:T(8,128)(2,1)S(1)} %bitcast.83, bf16[1,4,128,128]{3,2,0,1:T(8,128)(2,1)S(1)} %bitcast.85), kind=kLoop, calls=%fused_computation.19 | loop fusion | flops 786432 | bytes 1048576 | tf_op jit(solution)/shard_map/transpose | solution.py:58
  16.2 13.3 %all-to-all-start = ((bf16[4,4,128,128]{3,2,1,0:T(8,128)(2,1)}), bf16[4,4,128,128]{3,2,1,0:T(8,128)(2,1)S(1)}, u32[]{:S(2)}, u32[]{:S(2)}) async-start(bf16[4,4,128,128]{3,2,1,0:T(8,128)(2,1)} %maximum_bitcast_fusion), calls=%async_computation | async-start | bytes 1048576 | tf_op jit(solution)/shard_map/all_to_all | solution.py:59
  29.6 0.2 copy.25
  29.8 0.2 copy.24
  30.0 22.9 %all-to-all-done = bf16[4,4,128,128]{3,2,1,0:T(8,128)(2,1)S(1)} async-done(((bf16[4,4,128,128]{3,2,1,0:T(8,128)(2,1)}), bf16[4,4,128,128]{3,2,1,0:T(8,128)(2,1)S(1)}, u32[]{:S(2)}, u32[]{:S(2)}) %all-to-all-start) | async-done | bytes 524320 | tf_op jit(solution)/shard_map/all_to_all | solution.py:59
  53.0 0.2 convolution_bitcast_fusion.2
  53.2 0.2 fusion.3
  53.5 0.2 convolution_bitcast_fusion
  53.8 0.2 fusion.2
  54.1 18.0 %all_to_all.10 = bf16[4,2,128,128]{3,2,1,0:T(8,128)(2,1)S(1)} all-to-all(bf16[4,2,128,128]{3,2,1,0:T(8,128)(2,1)S(1)} %maximum_bitcast_fusion.1), channel_id=1, replica_groups=mesh['row'=192,'col'=4] {'col'}, dimensions={0} | all-to-all | bytes 524288 | tf_op jit(solution)/shard_map/all_to_all | solution.py:78
  72.2 0.7 fusion.21
  (19 shorter events, 0.3 us)
Async XLA Ops:
  3.3 7.8 %collective-permute-start = (bf16[256,256]{1,0:T(8,128)(2,1)S(1)}, bf16[256,256]{1,0:T(8,128)(2,1)S(1)}, u32[]{:S(2)}, u32[]{:S(2)}) collective-permute-start(bf16[256,256]{1,0:T(8,128)(2,1)S(1)} %get-tuple-element.6), channel_id=1, source_target_pairs={{0,4},{4,8},{8,12},{12,16},{16,20},{20,24},{24,28},{28,32},{32,36}... | collective-permute-start | bytes 393224 | tf_op jit(solution)/shard_map/ppermute | solution.py:12
  6.1 8.4 %collective-permute-start.1 = (bf16[256,256]{1,0:T(8,128)(2,1)S(1)}, bf16[256,256]{1,0:T(8,128)(2,1)S(1)}, u32[]{:S(2)}, u32[]{:S(2)}) collective-permute-start(bf16[256,256]{1,0:T(8,128)(2,1)S(1)} %get-tuple-element.7), channel_id=1, source_target_pairs={{4,0},{8,4},{12,8},{16,12},{20,16},{24,20},{28,24},{32,28},{36,32}... | collective-permute-start | bytes 393224 | tf_op jit(solution)/shard_map/ppermute | solution.py:12
  8.0 2.5 %copy-start.4 = (s32[512,16]{0,1:T(8,128)S(1)}, s32[512,16]{0,1:T(8,128)}, u32[]{:S(2)}) copy-start(s32[512,16]{0,1:T(8,128)} %param.12) | copy-start | bytes 98308
  10.5 4.0 %copy-start.3 = (bf16[512,128]{1,0:T(8,128)(2,1)S(1)}, bf16[512,128]{1,0:T(8,128)(2,1)}, u32[]{:S(2)}) copy-start(bf16[512,128]{1,0:T(8,128)(2,1)} %param.7) | copy-start | bytes 393220
  14.5 0.9 %copy-start.2 = (bf16[512,128]{1,0:T(8,128)(2,1)S(1)}, bf16[512,128]{1,0:T(8,128)(2,1)}, u32[]{:S(2)}) copy-start(bf16[512,128]{1,0:T(8,128)(2,1)} %param.8) | copy-start | bytes 393220
  14.9 14.7 %copy-start = (bf16[512,512]{1,0:T(8,128)(2,1)S(1)}, bf16[512,512]{1,0:T(8,128)(2,1)}, u32[]{:S(2)}) copy-start(bf16[512,512]{1,0:T(8,128)(2,1)} %param.10) | copy-start | bytes 1572868
  14.9 14.9 %copy-start.1 = (bf16[512,512]{1,0:T(8,128)(2,1)S(1)}, bf16[512,512]{1,0:T(8,128)(2,1)}, u32[]{:S(2)}) copy-start(bf16[512,512]{1,0:T(8,128)(2,1)} %param.9) | copy-start | bytes 1572868
  16.2 36.7 %all-to-all-start = ((bf16[4,4,128,128]{3,2,1,0:T(8,128)(2,1)}), bf16[4,4,128,128]{3,2,1,0:T(8,128)(2,1)S(1)}, u32[]{:S(2)}, u32[]{:S(2)}) async-start(bf16[4,4,128,128]{3,2,1,0:T(8,128)(2,1)} %maximum_bitcast_fusion), calls=%async_computation | async-start | bytes 1048576 | tf_op jit(solution)/shard_map/all_to_all | solution.py:59

commit v10 on v8

--- a/solution.py
+++ b/solution.py
@@ -69,8 +69,13 @@
             x, w, (((0, 2), (0, 1)), ((), ())), preferred_element_type=jnp.float32
         )
 
-    output = project(own_in[:, :, 0], ws) + project(agg_in[:, :, 0], wn)
-    feature_grad = project(own_in[:, :, 1], ws_t) + project(agg_in[:, :, 1], wn_t)
+    def project_both(x, w):
+        return lax.dot_general(
+            x, w, (((0, 2, 3), (0, 1, 2)), ((), ())), preferred_element_type=jnp.float32
+        )
+
+    output = project_both(ins[:, :, 0::2], jnp.stack([ws, wn], axis=1))
+    feature_grad = project_both(ins[:, :, 1::2], jnp.stack([ws_t, wn_t], axis=1))
     both = jnp.stack(
         [output.astype(jnp.bfloat16), feature_grad.astype(jnp.bfloat16)], axis=0
     )

time: 72.7 us -> 73.5 us (1.011)
  the two profiles are of different devices: /device:TPU:71 before, /device:TPU:99 now
where the time goes in v10:
time: 73.5 us; the launch traced here: 73.2 us
  waiting for transfers between devices  25.6 us (35%)
  starting transfers between devices  18.9 us (26%)
  blocking collectives  18.7 us (25%)
  other arithmetic  4.15 us (6%)
  local copies, waits for them, and re-layouts  3.43 us (5%)
  matrix products  1.56 us (2%)
  between operations  0.82 us (1%)
    all_to_all x1, waiting for transfers between devices, swap_chunks(): return lax.all_to_all(block, axis, 0, 0, tiled=True)  24.3 us
    all_to_all x1, blocking collectives, per_device(): back = lax.all_to_all(both, 'col', 0, 0, tiled=True)  18.7 us
    all_to_all x1, starting transfers between devices, swap_chunks(): return lax.all_to_all(block, axis, 0, 0, tiled=True)  13.3 us
    ppermute x2, starting transfers between devices, shifted(): return lax.ppermute(block, axis, route)  5.6 us
    convert_element_type x1, other arithmetic, per_device(): tile_rows.astype(jnp.bfloat16).reshape(blocks_here, block, -1, block)  2.47 us
    unnamed x9, local copies, waits for them, and re-layouts  2.14 us
  transfers between devices with their start and end apart: 3, of which 2 were waited for; matrix products, arithmetic and copies ran while one was open for 5% of the time, Pallas kernels for 0%

profile of v10, /device:TPU:99, one launch (start us, length us, event | category | flops | bytes accessed | tf_op | source)
XLA Modules:
  0.0 73.2 jit_solution(17957830012840594581)
XLA Ops:
  0.6 1.0 %copy.34 = bf16[512,128]{0,1:T(8,128)(2,1)S(1)} copy(bf16[512,128]{1,0:T(8,128)(2,1)} %param.8) | data formatting | bytes 262144 | tf_op args[1]
  1.6 0.7 convert_divide_fusion
  2.3 1.0 %copy.33 = bf16[512,128]{0,1:T(8,128)(2,1)S(1)} copy(bf16[512,128]{1,0:T(8,128)(2,1)} %param.7) | data formatting | bytes 262144 | tf_op args[0]
  3.4 3.7 %collective-permute-start = (bf16[256,256]{0,1:T(8,128)(2,1)S(1)}, bf16[256,256]{0,1:T(8,128)(2,1)S(1)}, u32[]{:S(2)}, u32[]{:S(2)}) collective-permute-start(bf16[256,256]{0,1:T(8,128)(2,1)S(1)} %get-tuple-element.4), channel_id=1, source_target_pairs={{0,4},{4,8},{8,12},{12,16},{16,20},{20,24},{24,28},{28,32},{32,36}... | collective-permute-start | bytes 393224 | tf_op jit(solution)/shard_map/ppermute | solution.py:12
  7.1 1.9 %collective-permute-start.1 = (bf16[256,256]{0,1:T(8,128)(2,1)S(1)}, bf16[256,256]{0,1:T(8,128)(2,1)S(1)}, u32[]{:S(2)}, u32[]{:S(2)}) collective-permute-start(bf16[256,256]{0,1:T(8,128)(2,1)S(1)} %get-tuple-element.5), channel_id=1, source_target_pairs={{4,0},{8,4},{12,8},{16,12},{20,16},{24,20},{28,24},{32,28},{36,32}... | collective-permute-start | bytes 393224 | tf_op jit(solution)/shard_map/ppermute | solution.py:12
  9.0 0.0 copy-start.2
  9.0 2.5 %convert_element_type.29 = bf16[512,16,128]{2,1,0:T(8,128)(2,1)S(1)} convert(s32[512,16,128]{2,1,0:T(8,128)} %param.11) | non-fusion elementwise | flops 1048576 | bytes 6291456 | tf_op jit(solution)/shard_map/convert_element_type | solution.py:51
  11.5 0.0 copy-done.2
  11.5 0.1 copy.45
  11.6 0.4 convolution_convert_fusion
  12.1 0.0 collective-permute-done
  12.1 1.3 %collective-permute-done.1 = bf16[256,256]{0,1:T(8,128)(2,1)S(1)} collective-permute-done((bf16[256,256]{0,1:T(8,128)(2,1)S(1)}, bf16[256,256]{0,1:T(8,128)(2,1)S(1)}, u32[]{:S(2)}, u32[]{:S(2)}) %collective-permute-start.1) | collective-permute-done | bytes 131104 | tf_op jit(solution)/shard_map/ppermute | solution.py:12
  13.4 0.5 fusion.2
  13.9 0.0 copy-start.1
  13.9 0.0 copy-start
  13.9 0.9 %copy_bitcast_fusion = bf16[4,128,512]{1,2,0:T(8,128)(2,1)} fusion(bf16[512,128]{0,1:T(8,128)(2,1)S(1)} %slice.58, bf16[512,128]{0,1:T(8,128)(2,1)S(1)} %fusion.18, bf16[512,128]{0,1:T(8,128)(2,1)S(1)} %copy.34, bf16[512,128]{0,1:T(8,128)(2,1)S(1)} %copy.33), kind=kLoop, calls=%fused_computation.14 | loop fusion | flops 2097152 | bytes 1048576 | tf_op jit(solution)/shard_map/all_to_all | solution.py:18
  14.8 13.3 %all-to-all-start = ((bf16[4,128,512]{1,2,0:T(8,128)(2,1)}), bf16[4,128,512]{1,2,0:T(8,128)(2,1)S(1)}, u32[]{:S(2)}, u32[]{:S(2)}) async-start(bf16[4,128,512]{1,2,0:T(8,128)(2,1)} %copy_bitcast_fusion), calls=%async_computation | async-start | bytes 1048576 | tf_op jit(solution)/shard_map/all_to_all | solution.py:18
  28.2 0.2 copy.38
  28.4 0.2 copy.39
  28.6 24.3 %all-to-all-done = bf16[4,128,512]{1,2,0:T(8,128)(2,1)S(1)} async-done(((bf16[4,128,512]{1,2,0:T(8,128)(2,1)}), bf16[4,128,512]{1,2,0:T(8,128)(2,1)S(1)}, u32[]{:S(2)}, u32[]{:S(2)}) %all-to-all-start) | async-done | bytes 524320 | tf_op jit(solution)/shard_map/all_to_all | solution.py:18
  52.9 0.3 fusion
  53.3 0.3 fusion.1
  53.7 18.7 %all_to_all.14 = bf16[4,2,128,128]{3,2,1,0:T(8,128)(2,1)S(1)} all-to-all(bf16[4,2,128,128]{3,2,1,0:T(8,128)(2,1)S(1)} %maximum_bitcast_fusion.1), channel_id=1, replica_groups=mesh['row'=192,'col'=4] {'col'}, dimensions={0} | all-to-all | bytes 524288 | tf_op jit(solution)/shard_map/all_to_all | solution.py:83
  72.5 0.7 fusion.28
  (13 shorter events, 0.3 us)
Async XLA Ops:
  3.4 8.7 %collective-permute-start = (bf16[256,256]{0,1:T(8,128)(2,1)S(1)}, bf16[256,256]{0,1:T(8,128)(2,1)S(1)}, u32[]{:S(2)}, u32[]{:S(2)}) collective-permute-start(bf16[256,256]{0,1:T(8,128)(2,1)S(1)} %get-tuple-element.4), channel_id=1, source_target_pairs={{0,4},{4,8},{8,12},{12,16},{16,20},{20,24},{24,28},{28,32},{32,36}... | collective-permute-start | bytes 393224 | tf_op jit(solution)/shard_map/ppermute | solution.py:12
  7.1 6.3 %collective-permute-start.1 = (bf16[256,256]{0,1:T(8,128)(2,1)S(1)}, bf16[256,256]{0,1:T(8,128)(2,1)S(1)}, u32[]{:S(2)}, u32[]{:S(2)}) collective-permute-start(bf16[256,256]{0,1:T(8,128)(2,1)S(1)} %get-tuple-element.5), channel_id=1, source_target_pairs={{4,0},{8,4},{12,8},{16,12},{20,16},{24,20},{28,24},{32,28},{36,32}... | collective-permute-start | bytes 393224 | tf_op jit(solution)/shard_map/ppermute | solution.py:12
  9.0 2.5 %copy-start.2 = (s32[512,16]{0,1:T(8,128)S(1)}, s32[512,16]{0,1:T(8,128)}, u32[]{:S(2)}) copy-start(s32[512,16]{0,1:T(8,128)} %param.12) | copy-start | bytes 98308
  13.9 14.3 %copy-start.1 = (bf16[512,512]{1,0:T(8,128)(2,1)S(1)}, bf16[512,512]{1,0:T(8,128)(2,1)}, u32[]{:S(2)}) copy-start(bf16[512,512]{1,0:T(8,128)(2,1)} %param.9) | copy-start | bytes 1572868
  13.9 14.5 %copy-start = (bf16[512,512]{1,0:T(8,128)(2,1)S(1)}, bf16[512,512]{1,0:T(8,128)(2,1)}, u32[]{:S(2)}) copy-start(bf16[512,512]{1,0:T(8,128)(2,1)} %param.10) | copy-start | bytes 1572868
  14.8 38.1 %all-to-all-start = ((bf16[4,128,512]{1,2,0:T(8,128)(2,1)}), bf16[4,128,512]{1,2,0:T(8,128)(2,1)S(1)}, u32[]{:S(2)}, u32[]{:S(2)}) async-start(bf16[4,128,512]{1,2,0:T(8,128)(2,1)} %copy_bitcast_fusion), calls=%async_computation | async-start | bytes 1048576 | tf_op jit(solution)/shard_map/all_to_all | solution.py:18
